TPU v7x, 32 devices: a whole 2x2x4 slice. The times are simulated.
32 devices in a mesh: groups: 2 (over y), section: 4 (over x, core), filt: 4 (over z).
Axes of the slice: x: 2, y: 2, z: 4, core: 2. Of those that a mesh axis runs over, the one named last changes fastest.
Arguments:
- volumes: bfloat16 [16, 256, 4, 2, 128], P('groups', 'filt'), parts along dimension 0, may hold values from -6 to 6
- weights: bfloat16 [4, 256, 27, 256], P('section', 'filt'), may hold values from -0.125 to 0.125
- biases: float32 [4, 256], P('section', 'filt'), may hold values from -3 to 3
- cotangent: bfloat16 [16, 256, 4, 2, 128], P('groups', 'filt'), parts along dimension 0, may hold values from -6 to 6
Outputs:
- grad_weights: float32 [8, 256, 27, 256], P(('groups', 'section'), 'filt'), parts along dimension 0
- grad_biases: float32 [8, 256], P(('groups', 'section'), 'filt'), parts along dimension 0
- grad_inputs: bfloat16 [8, 8, 256, 4, 2, 128], P(('groups', 'section'), None, 'filt'), parts along dimension 0
There are 2 independent parts, one for each index of `groups`. A program takes and returns all parts, laid end to end along the dimension named above; an argument that names none is the same for every part. Nothing has to cross between parts.
All inputs are finite; a program needn't handle non-finite values.
Results may differ from a plain program's by a relative error of at most 0.019.
Values may be sent and summed in bfloat16 or wider, within the bound.
No kernel may reach another device: no remote copies, remote signals or barrier semaphores. Data moves between devices by JAX's collectives and lax.ppermute only.
A program may use at most 64 MiB of HBM per device.

v0:
```python
import math

import jax
import jax.numpy as jnp
import numpy as np
from jax import lax
from jax.sharding import PartitionSpec as P

tap_offsets = [
    (first, second, third) for first in (-1, 0, 1) for second in (-1, 0, 1) for third in (-1, 0, 1)
]


def passed_along(value, axis, steps):
    count = lax.axis_size(axis)
    first, last = (max(0, -steps), min(count, count - steps))
    return lax.ppermute(value, axis, [(source, source + steps) for source in range(first, last)])


def for_sending(x):
    return jax.tree.map(lambda a: a.astype(jnp.bfloat16) if a.dtype == jnp.float32 else a, x)


def lane_shift(values, step):
    if step == 0:
        return values
    width = values.shape[-1]
    source = jnp.arange(width)[:, None]
    target = jnp.arange(width)[None, :]
    if values.dtype == jnp.float32:
        matrix = (source == target + step).astype(jnp.float32)
        return jnp.einsum(
            "...z,zw->...w",
            values,
            matrix,
            precision=lax.Precision.HIGHEST,
            preferred_element_type=jnp.float32,
        )
    matrix = (source == target + step).astype(values.dtype)
    return jnp.einsum("...z,zw->...w", values, matrix, preferred_element_type=jnp.float32).astype(
        values.dtype
    )


def row_shift(values, step_x, step_y, extent_x, extent_y):
    if step_x == 0 and step_y == 0:
        return values
    row_total = extent_x * extent_y
    delta = step_x * extent_y + step_y
    keep_mask = np.zeros((row_total, 1), dtype=bool)
    for row_pos in range(row_total):
        pos_x = row_pos // extent_y + step_x
        pos_y = row_pos % extent_y + step_y
        keep_mask[row_pos, 0] = 0 <= pos_x < extent_x and 0 <= pos_y < extent_y
    margin = extent_y + 1
    padded = jnp.pad(values, [(0, 0)] * (values.ndim - 2) + [(margin, margin), (0, 0)])
    sliced = lax.slice_in_dim(
        padded, margin + delta, margin + delta + row_total, axis=values.ndim - 2
    )
    return jnp.where(jnp.asarray(keep_mask), sliced, jnp.zeros((), values.dtype))


def sum_taps(product, direction, extent_x, extent_y):
    summed = jnp.zeros(product.shape[:1] + product.shape[2:], jnp.float32)
    for lane_step in (-1, 0, 1):
        partial_sum = jnp.zeros(product.shape[:1] + product.shape[2:], jnp.float32)
        for tap_index, offset in enumerate(tap_offsets):
            if offset[2] == lane_step:
                partial_sum = partial_sum + row_shift(
                    product[:, tap_index],
                    direction * offset[0],
                    direction * offset[1],
                    extent_x,
                    extent_y,
                )
        summed = summed + lane_shift(partial_sum, direction * lane_step)
    return summed


def stack_taps(values, direction, extent_x, extent_y):
    shifted_lanes = {}
    for lane_step in (-1, 0, 1):
        shifted_lanes[lane_step] = lane_shift(values, direction * lane_step)
    return jnp.stack(
        [
            row_shift(
                shifted_lanes[offset[2]],
                direction * offset[0],
                direction * offset[1],
                extent_x,
                extent_y,
            )
            for offset in tap_offsets
        ],
        axis=1,
    )


def silu_slope(pre_act):
    sigmoid = jax.nn.sigmoid(pre_act)
    return sigmoid * (1.0 + pre_act * (1.0 - sigmoid))


def store_slot(buffer, entry, position, in_range):
    previous = lax.dynamic_index_in_dim(buffer, position, 0, keepdims=False)
    return lax.dynamic_update_index_in_dim(
        buffer, jnp.where(in_range, entry, previous), position, 0
    )


def local(volumes, weights, biases, cotangent):
    section_count = lax.axis_size("section")
    section_pos = lax.axis_index("section")
    micro_count = volumes.shape[0]
    tick_count = micro_count + section_count - 1
    weight = weights[0]
    own_count, tap_count, channels = weight.shape
    weight_rows = weight.reshape(own_count * tap_count, channels)
    layer_bias = biases[0]
    extent_x, extent_y, lane_count = volumes.shape[2:]
    row_total = extent_x * extent_y
    cell_count = row_total * lane_count
    flat_volumes = volumes.reshape(micro_count, own_count, row_total, lane_count)
    flat_cotangent = cotangent.reshape(micro_count, own_count, row_total, lane_count)
    stored = jnp.zeros((micro_count, own_count, row_total, lane_count), jnp.bfloat16)
    saved_pre = jnp.zeros((micro_count, own_count, row_total, lane_count), jnp.float32)
    empty_slab = jnp.zeros((own_count, row_total, lane_count), jnp.bfloat16)

    def forward_tick(tick_now, carried):
        incoming, saved_pre, stored = carried
        sample = tick_now - section_pos
        in_range = (sample >= 0) & (sample < micro_count)
        position = jnp.clip(sample, 0, micro_count - 1)
        first_input = lax.dynamic_index_in_dim(flat_volumes, position, 0, keepdims=False)
        own_input = jnp.where(section_pos == 0, first_input, incoming)
        panel_part = jax.tree.map(
            lambda a: lax.all_gather(a, "filt", axis=0, tiled=True), own_input
        )
        columns = lax.slice_in_dim(weight_rows, 0, panel_part.shape[0], axis=1)
        product = jnp.zeros(
            (own_count * tap_count, row_total, lane_count), jnp.float32
        ) + jnp.einsum("ki,irz->krz", columns, panel_part, preferred_element_type=jnp.float32)
        stored = store_slot(stored, own_input, position, in_range)
        pre_act = (
            sum_taps(
                product.reshape(own_count, tap_count, row_total, lane_count), 1, extent_x, extent_y
            )
            + layer_bias[:, None, None]
        )
        saved_pre = store_slot(saved_pre, pre_act, position, in_range)
        outgoing = jax.nn.silu(pre_act).astype(jnp.bfloat16)
        incoming = passed_along(outgoing, "section", 1)
        return (incoming, saved_pre, stored)

    unused_slab, saved_pre, stored = lax.fori_loop(
        0, tick_count, forward_tick, (empty_slab, saved_pre, stored)
    )

    def backward_tick(tick_now, carried):
        incoming, grad_rows, grad_bias, grad_in = carried
        sample = tick_now - (section_count - 1 - section_pos)
        in_range = (sample >= 0) & (sample < micro_count)
        position = jnp.clip(sample, 0, micro_count - 1)
        last_grad = lax.dynamic_index_in_dim(flat_cotangent, position, 0, keepdims=False)
        upstream = jnp.where(section_pos == section_count - 1, last_grad, incoming)
        pre_act = lax.dynamic_index_in_dim(saved_pre, position, 0, keepdims=False)
        slope_grad = (upstream.astype(jnp.float32) * silu_slope(pre_act)).astype(jnp.bfloat16)
        stacked = stack_taps(slope_grad, -1, extent_x, extent_y).reshape(
            own_count * tap_count, row_total, lane_count
        )
        own_input = lax.dynamic_index_in_dim(stored, position, 0, keepdims=False)
        weight_term = jnp.einsum(
            "krz,irz->ki",
            stacked,
            lax.all_gather(for_sending(own_input), "filt", axis=0, tiled=True),
            preferred_element_type=jnp.float32,
        )
        grad_rows = grad_rows + jnp.where(in_range, weight_term, 0.0)
        grad_bias = grad_bias + jnp.where(
            in_range, jnp.sum(slope_grad.astype(jnp.float32), axis=(1, 2)), 0.0
        )
        columns = lax.slice_in_dim(weight_rows, 0, own_count * lax.axis_size("filt"), axis=1)
        input_grad = lax.psum_scatter(
            jnp.einsum("ki,krz->irz", columns, stacked, preferred_element_type=jnp.float32).astype(
                jnp.bfloat16
            ),
            "filt",
            scatter_dimension=0,
            tiled=True,
        ).astype(jnp.float32)
        input_grad = input_grad.astype(jnp.bfloat16)
        grad_in = store_slot(grad_in, input_grad, position, in_range)
        incoming = passed_along(input_grad, "section", -1)
        return (incoming, grad_rows, grad_bias, grad_in)

    start_state = (
        empty_slab,
        jnp.zeros((own_count * tap_count, channels), jnp.float32),
        jnp.zeros((own_count,), jnp.float32),
        jnp.zeros((micro_count, own_count, row_total, lane_count), jnp.bfloat16),
    )
    unused_grad, grad_rows, grad_bias, grad_in = lax.fori_loop(
        0, tick_count, backward_tick, start_state
    )
    norm_scale = 1.0 / math.sqrt(micro_count * cell_count)
    grad_out = grad_in.reshape(1, micro_count, own_count, extent_x, extent_y, lane_count)
    return (
        (grad_rows * norm_scale).reshape(1, own_count, tap_count, channels),
        (grad_bias * norm_scale)[None],
        grad_out,
    )


def solution(mesh):
    in_specs = (
        P("groups", "filt", None, None, None),
        P("section", "filt", None, None),
        P("section", "filt"),
        P("groups", "filt", None, None, None),
    )
    out_specs = (
        P(("groups", "section"), "filt", None, None),
        P(("groups", "section"), "filt"),
        P(("groups", "section"), None, "filt", None, None, None),
    )
    return jax.shard_map(local, mesh=mesh, in_specs=in_specs, out_specs=out_specs, check_vma=False)
```

profile of v0, /device:TPU:1, one launch (start us, length us, event | category | flops | bytes accessed | tf_op | source)
XLA Modules:
  0.0 1059.6 jit_solution(5570250423504639003)
XLA Ops:
  13.4 434.8 %while.45 = (s32[]{:T(128)}, bf16[64,8,128]{2,0,1:T(8,128)(2,1)S(1)}, f32[8,64,8,128]{3,1,2,0:T(8,128)}, bf16[8,64,8,128]{3,1,2,0:T(8,128)(2,1)}, pred[]{:T(512)...) while((s32[]{:T(128)}, ...), condition=%wide.region_1.2_spmd.clone.clone, body=%wide.region_0.1_spmd.sunk.clone.clone.sunk | while | flops 1111195904 | bytes 60796016 | solution.py:155
  15.1 15.3 %all_gather.26 = bf16[256,8,128]{2,0,1:T(8,128)(2,1)S(1)} all-gather(bf16[64,8,128]{2,0,1:T(8,128)(2,1)S(1)} %get-tuple-element.2151), channel_id=1, replica_groups=mesh['groups'=2,'section'=4,'filt'=4] {'filt'}, dimensions={0}, use_global_device_ids=true | all-gather | bytes 655360 | tf_op jit(solution)/shard_map/while/body/eval_jaxpr/all_gather | solution.py:137
  32.7 9.4 copy.273
  46.7 5.1 collective-permute-start
  55.4 14.9 %all_gather.26 = bf16[256,8,128]{2,0,1:T(8,128)(2,1)S(1)} all-gather(bf16[64,8,128]{2,0,1:T(8,128)(2,1)S(1)} %get-tuple-element.2151), channel_id=1, replica_groups=mesh['groups'=2,'section'=4,'filt'=4] {'filt'}, dimensions={0}, use_global_device_ids=true | all-gather | bytes 655360 | tf_op jit(solution)/shard_map/while/body/eval_jaxpr/all_gather | solution.py:137
  72.6 9.4 copy.273
  86.6 5.8 collective-permute-start
  95.9 13.3 %all_gather.26 = bf16[256,8,128]{2,0,1:T(8,128)(2,1)S(1)} all-gather(bf16[64,8,128]{2,0,1:T(8,128)(2,1)S(1)} %get-tuple-element.2151), channel_id=1, replica_groups=mesh['groups'=2,'section'=4,'filt'=4] {'filt'}, dimensions={0}, use_global_device_ids=true | all-gather | bytes 655360 | tf_op jit(solution)/shard_map/while/body/eval_jaxpr/all_gather | solution.py:137
  111.5 9.4 copy.273
  125.6 6.9 collective-permute-start
  136.1 13.0 %all_gather.26 = bf16[256,8,128]{2,0,1:T(8,128)(2,1)S(1)} all-gather(bf16[64,8,128]{2,0,1:T(8,128)(2,1)S(1)} %get-tuple-element.2151), channel_id=1, replica_groups=mesh['groups'=2,'section'=4,'filt'=4] {'filt'}, dimensions={0}, use_global_device_ids=true | all-gather | bytes 655360 | tf_op jit(solution)/shard_map/while/body/eval_jaxpr/all_gather | solution.py:137
  151.3 9.4 copy.273
  165.4 6.2 collective-permute-start
  175.2 12.9 %all_gather.26 = bf16[256,8,128]{2,0,1:T(8,128)(2,1)S(1)} all-gather(bf16[64,8,128]{2,0,1:T(8,128)(2,1)S(1)} %get-tuple-element.2151), channel_id=1, replica_groups=mesh['groups'=2,'section'=4,'filt'=4] {'filt'}, dimensions={0}, use_global_device_ids=true | all-gather | bytes 655360 | tf_op jit(solution)/shard_map/while/body/eval_jaxpr/all_gather | solution.py:137
  190.3 9.4 copy.273
  204.3 6.6 collective-permute-start
  214.5 12.4 %all_gather.26 = bf16[256,8,128]{2,0,1:T(8,128)(2,1)S(1)} all-gather(bf16[64,8,128]{2,0,1:T(8,128)(2,1)S(1)} %get-tuple-element.2151), channel_id=1, replica_groups=mesh['groups'=2,'section'=4,'filt'=4] {'filt'}, dimensions={0}, use_global_device_ids=true | all-gather | bytes 655360 | tf_op jit(solution)/shard_map/while/body/eval_jaxpr/all_gather | solution.py:137
  229.2 9.4 copy.273
  243.2 6.8 collective-permute-start
  253.6 13.0 %all_gather.26 = bf16[256,8,128]{2,0,1:T(8,128)(2,1)S(1)} all-gather(bf16[64,8,128]{2,0,1:T(8,128)(2,1)S(1)} %get-tuple-element.2151), channel_id=1, replica_groups=mesh['groups'=2,'section'=4,'filt'=4] {'filt'}, dimensions={0}, use_global_device_ids=true | all-gather | bytes 655360 | tf_op jit(solution)/shard_map/while/body/eval_jaxpr/all_gather | solution.py:137
  268.9 9.4 copy.273
  282.9 6.5 collective-permute-start
  293.0 12.6 %all_gather.26 = bf16[256,8,128]{2,0,1:T(8,128)(2,1)S(1)} all-gather(bf16[64,8,128]{2,0,1:T(8,128)(2,1)S(1)} %get-tuple-element.2151), channel_id=1, replica_groups=mesh['groups'=2,'section'=4,'filt'=4] {'filt'}, dimensions={0}, use_global_device_ids=true | all-gather | bytes 655360 | tf_op jit(solution)/shard_map/while/body/eval_jaxpr/all_gather | solution.py:137
  307.8 9.4 copy.273
  321.8 6.6 collective-permute-start
  332.1 12.6 %all_gather.26 = bf16[256,8,128]{2,0,1:T(8,128)(2,1)S(1)} all-gather(bf16[64,8,128]{2,0,1:T(8,128)(2,1)S(1)} %get-tuple-element.2151), channel_id=1, replica_groups=mesh['groups'=2,'section'=4,'filt'=4] {'filt'}, dimensions={0}, use_global_device_ids=true | all-gather | bytes 655360 | tf_op jit(solution)/shard_map/while/body/eval_jaxpr/all_gather | solution.py:137
  346.9 9.4 copy.273
  360.9 6.9 collective-permute-start
  371.4 12.2 %all_gather.26 = bf16[256,8,128]{2,0,1:T(8,128)(2,1)S(1)} all-gather(bf16[64,8,128]{2,0,1:T(8,128)(2,1)S(1)} %get-tuple-element.2151), channel_id=1, replica_groups=mesh['groups'=2,'section'=4,'filt'=4] {'filt'}, dimensions={0}, use_global_device_ids=true | all-gather | bytes 655360 | tf_op jit(solution)/shard_map/while/body/eval_jaxpr/all_gather | solution.py:137
  385.8 9.4 copy.273
  399.9 7.0 collective-permute-start
  410.5 12.2 %all_gather.26 = bf16[256,8,128]{2,0,1:T(8,128)(2,1)S(1)} all-gather(bf16[64,8,128]{2,0,1:T(8,128)(2,1)S(1)} %get-tuple-element.2151), channel_id=1, replica_groups=mesh['groups'=2,'section'=4,'filt'=4] {'filt'}, dimensions={0}, use_global_device_ids=true | all-gather | bytes 655360 | tf_op jit(solution)/shard_map/while/body/eval_jaxpr/all_gather | solution.py:137
  425.0 9.4 copy.273
  439.0 7.2 collective-permute-start
  449.3 596.6 %while.46 = (s32[]{:T(128)}, bf16[64,8,128]{2,1,0:T(8,128)(2,1)S(1)}, f32[1728,256]{1,0:T(8,128)}, f32[64]{0:T(128)}, bf16[8,64,8,128]{3,2,1,0:T(8,128)(2,1)}, /...) while((s32[]{:T(128)}, ...), condition=%wide.region_5.6_spmd.clone.clone.clone, body=%wide.region_2.5_spmd.sunk.clone.clone.clone.sunk | while | flops 1849737728 | bytes 33530844 | solution.py:202
  472.5 18.2 %all-gather.4 = bf16[1,256,8,128]{3,1,2,0:T(8,128)(2,1)S(1)} all-gather(bf16[1,64,8,128]{3,1,2,0:T(8,128)(2,1)} %constant_dynamic-slice_fusion.13), channel_id=2, replica_groups=mesh['groups'=2,'section'=4,'filt'=4] {'filt'}, dimensions={1}, use_global_device_ids=true | all-gather | bytes 655360 | tf_op jit(solution)/shard_map/while/body/eval_jaxpr/all_gather | solution.py:175
  498.0 4.9 collective-permute-done.1
  525.9 20.0 %all-gather.4 = bf16[1,256,8,128]{3,1,2,0:T(8,128)(2,1)S(1)} all-gather(bf16[1,64,8,128]{3,1,2,0:T(8,128)(2,1)} %constant_dynamic-slice_fusion.13), channel_id=2, replica_groups=mesh['groups'=2,'section'=4,'filt'=4] {'filt'}, dimensions={1}, use_global_device_ids=true | all-gather | bytes 655360 | tf_op jit(solution)/shard_map/while/body/eval_jaxpr/all_gather | solution.py:175
  580.5 20.0 %all-gather.4 = bf16[1,256,8,128]{3,1,2,0:T(8,128)(2,1)S(1)} all-gather(bf16[1,64,8,128]{3,1,2,0:T(8,128)(2,1)} %constant_dynamic-slice_fusion.13), channel_id=2, replica_groups=mesh['groups'=2,'section'=4,'filt'=4] {'filt'}, dimensions={1}, use_global_device_ids=true | all-gather | bytes 655360 | tf_op jit(solution)/shard_map/while/body/eval_jaxpr/all_gather | solution.py:175
  635.1 19.3 %all-gather.4 = bf16[1,256,8,128]{3,1,2,0:T(8,128)(2,1)S(1)} all-gather(bf16[1,64,8,128]{3,1,2,0:T(8,128)(2,1)} %constant_dynamic-slice_fusion.13), channel_id=2, replica_groups=mesh['groups'=2,'section'=4,'filt'=4] {'filt'}, dimensions={1}, use_global_device_ids=true | all-gather | bytes 655360 | tf_op jit(solution)/shard_map/while/body/eval_jaxpr/all_gather | solution.py:175
  689.0 20.1 %all-gather.4 = bf16[1,256,8,128]{3,1,2,0:T(8,128)(2,1)S(1)} all-gather(bf16[1,64,8,128]{3,1,2,0:T(8,128)(2,1)} %constant_dynamic-slice_fusion.13), channel_id=2, replica_groups=mesh['groups'=2,'section'=4,'filt'=4] {'filt'}, dimensions={1}, use_global_device_ids=true | all-gather | bytes 655360 | tf_op jit(solution)/shard_map/while/body/eval_jaxpr/all_gather | solution.py:175
  743.7 19.2 %all-gather.4 = bf16[1,256,8,128]{3,1,2,0:T(8,128)(2,1)S(1)} all-gather(bf16[1,64,8,128]{3,1,2,0:T(8,128)(2,1)} %constant_dynamic-slice_fusion.13), channel_id=2, replica_groups=mesh['groups'=2,'section'=4,'filt'=4] {'filt'}, dimensions={1}, use_global_device_ids=true | all-gather | bytes 655360 | tf_op jit(solution)/shard_map/while/body/eval_jaxpr/all_gather | solution.py:175
  797.5 20.0 %all-gather.4 = bf16[1,256,8,128]{3,1,2,0:T(8,128)(2,1)S(1)} all-gather(bf16[1,64,8,128]{3,1,2,0:T(8,128)(2,1)} %constant_dynamic-slice_fusion.13), channel_id=2, replica_groups=mesh['groups'=2,'section'=4,'filt'=4] {'filt'}, dimensions={1}, use_global_device_ids=true | all-gather | bytes 655360 | tf_op jit(solution)/shard_map/while/body/eval_jaxpr/all_gather | solution.py:175
  818.7 3.8 fusion.217
  852.1 19.3 %all-gather.4 = bf16[1,256,8,128]{3,1,2,0:T(8,128)(2,1)S(1)} all-gather(bf16[1,64,8,128]{3,1,2,0:T(8,128)(2,1)} %constant_dynamic-slice_fusion.13), channel_id=2, replica_groups=mesh['groups'=2,'section'=4,'filt'=4] {'filt'}, dimensions={1}, use_global_device_ids=true | all-gather | bytes 655360 | tf_op jit(solution)/shard_map/while/body/eval_jaxpr/all_gather | solution.py:175
  906.0 20.0 %all-gather.4 = bf16[1,256,8,128]{3,1,2,0:T(8,128)(2,1)S(1)} all-gather(bf16[1,64,8,128]{3,1,2,0:T(8,128)(2,1)} %constant_dynamic-slice_fusion.13), channel_id=2, replica_groups=mesh['groups'=2,'section'=4,'filt'=4] {'filt'}, dimensions={1}, use_global_device_ids=true | all-gather | bytes 655360 | tf_op jit(solution)/shard_map/while/body/eval_jaxpr/all_gather | solution.py:175
  960.7 19.2 %all-gather.4 = bf16[1,256,8,128]{3,1,2,0:T(8,128)(2,1)S(1)} all-gather(bf16[1,64,8,128]{3,1,2,0:T(8,128)(2,1)} %constant_dynamic-slice_fusion.13), channel_id=2, replica_groups=mesh['groups'=2,'section'=4,'filt'=4] {'filt'}, dimensions={1}, use_global_device_ids=true | all-gather | bytes 655360 | tf_op jit(solution)/shard_map/while/body/eval_jaxpr/all_gather | solution.py:175
  1014.4 20.0 %all-gather.4 = bf16[1,256,8,128]{3,1,2,0:T(8,128)(2,1)S(1)} all-gather(bf16[1,64,8,128]{3,1,2,0:T(8,128)(2,1)} %constant_dynamic-slice_fusion.13), channel_id=2, replica_groups=mesh['groups'=2,'section'=4,'filt'=4] {'filt'}, dimensions={1}, use_global_device_ids=true | all-gather | bytes 655360 | tf_op jit(solution)/shard_map/while/body/eval_jaxpr/all_gather | solution.py:175
  (796 shorter events, 498.7 us)
Async XLA Ops:
  7.2 3.1 copy-start
  8.9 4.4 copy-start.1
  9.0 4.4 copy-start.2
  9.0 4.4 copy-start.3
  9.0 4.4 copy-start.4
  9.0 4.4 copy-start.6
  46.7 7.0 collective-permute-start
  86.6 7.7 collective-permute-start
  125.6 8.9 collective-permute-start
  165.4 8.2 collective-permute-start
  204.3 8.5 collective-permute-start
  243.2 8.8 collective-permute-start
  282.9 8.4 collective-permute-start
  321.8 8.6 collective-permute-start
  360.9 8.8 collective-permute-start
  399.9 9.0 collective-permute-start
  439.0 9.2 collective-permute-start
  449.4 44.2 %reduce-scatter.2.cloned.1.call-start = ((), (), s32[]{:S(2)}) async-start(), calls=%async_computation.1 | async-start | bytes 655360 | tf_op jit(solution)/shard_map/while/body/eval_jaxpr/reduce_scatter | solution.py:183
  493.6 9.3 collective-permute-start.1
  502.9 48.1 %reduce-scatter.2.cloned.1.call-start = ((), (), s32[]{:S(2)}) async-start(), calls=%async_computation.1 | async-start | bytes 655360 | tf_op jit(solution)/shard_map/while/body/eval_jaxpr/reduce_scatter | solution.py:183
  551.0 6.5 collective-permute-start.1
  557.5 48.1 %reduce-scatter.2.cloned.1.call-start = ((), (), s32[]{:S(2)}) async-start(), calls=%async_computation.1 | async-start | bytes 655360 | tf_op jit(solution)/shard_map/while/body/eval_jaxpr/reduce_scatter | solution.py:183
  605.6 6.5 collective-permute-start.1
  612.1 47.4 %reduce-scatter.2.cloned.1.call-start = ((), (), s32[]{:S(2)}) async-start(), calls=%async_computation.1 | async-start | bytes 655360 | tf_op jit(solution)/shard_map/while/body/eval_jaxpr/reduce_scatter | solution.py:183
  659.5 6.5 collective-permute-start.1
  666.0 48.2 %reduce-scatter.2.cloned.1.call-start = ((), (), s32[]{:S(2)}) async-start(), calls=%async_computation.1 | async-start | bytes 655360 | tf_op jit(solution)/shard_map/while/body/eval_jaxpr/reduce_scatter | solution.py:183
  714.2 6.5 collective-permute-start.1
  720.7 47.3 %reduce-scatter.2.cloned.1.call-start = ((), (), s32[]{:S(2)}) async-start(), calls=%async_computation.1 | async-start | bytes 655360 | tf_op jit(solution)/shard_map/while/body/eval_jaxpr/reduce_scatter | solution.py:183
  767.9 6.5 collective-permute-start.1
  774.4 48.1 %reduce-scatter.2.cloned.1.call-start = ((), (), s32[]{:S(2)}) async-start(), calls=%async_computation.1 | async-start | bytes 655360 | tf_op jit(solution)/shard_map/while/body/eval_jaxpr/reduce_scatter | solution.py:183
  822.6 6.5 collective-permute-start.1
  829.0 47.4 %reduce-scatter.2.cloned.1.call-start = ((), (), s32[]{:S(2)}) async-start(), calls=%async_computation.1 | async-start | bytes 655360 | tf_op jit(solution)/shard_map/while/body/eval_jaxpr/reduce_scatter | solution.py:183
  876.5 6.5 collective-permute-start.1
  883.0 48.1 %reduce-scatter.2.cloned.1.call-start = ((), (), s32[]{:S(2)}) async-start(), calls=%async_computation.1 | async-start | bytes 655360 | tf_op jit(solution)/shard_map/while/body/eval_jaxpr/reduce_scatter | solution.py:183
  931.1 6.5 collective-permute-start.1
  937.6 47.3 %reduce-scatter.2.cloned.1.call-start = ((), (), s32[]{:S(2)}) async-start(), calls=%async_computation.1 | async-start | bytes 655360 | tf_op jit(solution)/shard_map/while/body/eval_jaxpr/reduce_scatter | solution.py:183
  984.9 6.5 collective-permute-start.1
  991.4 48.1 %reduce-scatter.2.cloned.1.call-start = ((), (), s32[]{:S(2)}) async-start(), calls=%async_computation.1 | async-start | bytes 655360 | tf_op jit(solution)/shard_map/while/body/eval_jaxpr/reduce_scatter | solution.py:183
  1039.5 6.5 collective-permute-start.1
  1048.8 3.8 copy-start.5
Sparse Core Ops, SparseCore 0:
  469.5 23.8 reduce-scatter.1
  522.9 23.7 reduce-scatter.1
  577.5 22.9 reduce-scatter.1
  632.1 22.2 reduce-scatter.1
  686.0 23.0 reduce-scatter.1
  740.7 21.9 reduce-scatter.1
  794.5 22.9 reduce-scatter.1
  849.1 22.2 reduce-scatter.1
  903.0 22.9 reduce-scatter.1
  957.7 21.8 reduce-scatter.1
  1011.4 22.9 reduce-scatter.1
where the time goes:
time: 1070 us; the launch traced here: 1060 us
  blocking collectives  360 us (34%)
  local copies, waits for them, and re-layouts  233 us (22%)
  other arithmetic  189 us (18%)
  matrix products  132 us (12%)
  starting transfers between devices  93.6 us (9%)
  waiting for transfers between devices  36.5 us (3%)
  between operations  13.8 us (1%)
    all_gather x11, blocking collectives, backward_tick(): lax.all_gather(for_sending(own_input), 'filt', axis=0, tiled=True)  215 us
    all_gather x11, blocking collectives, forward_tick(): lax.all_gather(a, 'filt', axis=0, tiled=True)  144 us
    while x253, other arithmetic  107 us
    dot_general x11, local copies, waits for them, and re-layouts, forward_tick(): jnp.einsum('ki,irz->krz', columns, panel_part, preferred_element_type=jnp...  104 us
    ppermute x22, starting transfers between devices, passed_along(): lax.ppermute(value, axis, [(source, source + steps) for source in range(f...  93.5 us
    dot_general x11, matrix products, backward_tick(): jnp.einsum('krz,irz->ki', stacked, lax.all_gather(for_sending(own_input),...  40.4 us
    dynamic_slice x33, local copies, waits for them, and re-layouts, store_slot(): previous = lax.dynamic_index_in_dim(buffer, position, 0, keepdims=False)  38 us
    ppermute x22, waiting for transfers between devices, passed_along(): lax.ppermute(value, axis, [(source, source + steps) for source in range(f...  36.3 us
  transfers between devices with their start and end apart: 33, of which 22 were waited for; matrix products, arithmetic and copies ran while one was open for 12% of the time, Pallas kernels for 0%

commit v1 on v0

v1 whole, which is shorter than its diff:
```python
import math

import jax
import jax.numpy as jnp
from jax import lax
from jax.sharding import PartitionSpec as P

CHUNK = 1

PAD3 = ((1, 1), (1, 1), (1, 1))


def silu_slope(pre_act):
    sigmoid = jax.nn.sigmoid(pre_act)
    return sigmoid * (1.0 + pre_act * (1.0 - sigmoid))


def conv_forward(act, kernel):
    return lax.conv_general_dilated(
        act, kernel, (1, 1, 1), PAD3,
        dimension_numbers=("NCDHW", "ODHWI", "NCDHW"),
        preferred_element_type=jnp.float32,
    )


def conv_input_grad(slope, kernel):
    flipped = kernel[:, ::-1, ::-1, ::-1, :]
    return lax.conv_general_dilated(
        slope, flipped, (1, 1, 1), PAD3,
        dimension_numbers=("NCDHW", "IDHWO", "NCDHW"),
        preferred_element_type=jnp.float32,
    )


def conv_weight_grad(act, slope):
    return lax.conv_general_dilated(
        act, slope, (1, 1, 1), PAD3,
        dimension_numbers=("CNDHW", "IODHW", "CDHWN"),
        preferred_element_type=jnp.float32,
    )


def local(volumes, weights, biases, cotangent):
    section_count = lax.axis_size("section")
    section_pos = lax.axis_index("section")
    micro_count = volumes.shape[0]
    chunk = CHUNK if micro_count % CHUNK == 0 else 1
    chunk_count = micro_count // chunk
    tick_count = chunk_count + section_count - 1
    own_count, tap_count, channels = weights.shape[1:]
    extent = volumes.shape[2:]
    kernel = weights[0].reshape(own_count, 3, 3, 3, channels)
    layer_bias = biases[0][None, :, None, None, None]
    slab = (chunk, own_count) + tuple(extent)
    forward_pairs = [(i, i + 1) for i in range(section_count - 1)]
    backward_pairs = [(i + 1, i) for i in range(section_count - 1)]

    incoming = jnp.zeros(slab, jnp.bfloat16)
    gathered = []
    pres = []
    for tick in range(tick_count):
        if tick < chunk_count:
            first = volumes[tick * chunk:(tick + 1) * chunk]
        else:
            first = jnp.zeros(slab, jnp.bfloat16)
        own_input = jnp.where(section_pos == 0, first, incoming)
        full_input = lax.all_gather(own_input, "filt", axis=1, tiled=True)
        pre_act = conv_forward(full_input, kernel) + layer_bias
        gathered.append(full_input)
        pres.append(pre_act)
        if tick < tick_count - 1:
            outgoing = jax.nn.silu(pre_act).astype(jnp.bfloat16)
            incoming = lax.ppermute(outgoing, "section", forward_pairs)

    incoming = jnp.zeros(slab, jnp.bfloat16)
    grad_kernel = jnp.zeros((own_count, 3, 3, 3, channels), jnp.float32)
    grad_bias = jnp.zeros((own_count,), jnp.float32)
    results = []
    for tick in range(tick_count):
        forward_tick = tick_count - 1 - tick
        if tick < chunk_count:
            start = (chunk_count - 1 - tick) * chunk
            last = cotangent[start:start + chunk]
        else:
            last = jnp.zeros(slab, jnp.bfloat16)
        upstream = jnp.where(section_pos == section_count - 1, last, incoming)
        sample = forward_tick - section_pos
        in_range = (sample >= 0) & (sample < chunk_count)
        slope = (upstream.astype(jnp.float32) * silu_slope(pres[forward_tick])).astype(jnp.bfloat16)
        slope = jnp.where(in_range, slope, jnp.zeros((), jnp.bfloat16))
        grad_kernel = grad_kernel + conv_weight_grad(gathered[forward_tick], slope)
        grad_bias = grad_bias + jnp.sum(slope.astype(jnp.float32), axis=(0, 2, 3, 4))
        partial = jnp.moveaxis(conv_input_grad(slope, kernel).astype(jnp.bfloat16), 1, 0)
        partial = partial.reshape(channels, chunk * extent[0] * extent[1], extent[2])
        scattered = lax.psum_scatter(partial, "filt", scatter_dimension=0, tiled=True)
        input_grad = jnp.moveaxis(scattered.reshape((own_count, chunk) + tuple(extent)), 0, 1)
        results.append(input_grad)
        if tick < tick_count - 1:
            incoming = lax.ppermute(input_grad, "section", backward_pairs)

    reversed_results = jnp.stack(results[::-1])
    picked = lax.dynamic_slice_in_dim(reversed_results, section_pos, chunk_count, axis=0)
    grad_in = picked.reshape((1, micro_count, own_count) + tuple(extent))
    norm_scale = 1.0 / math.sqrt(micro_count * math.prod(extent))
    return (
        (grad_kernel * norm_scale).reshape(1, own_count, tap_count, channels),
        (grad_bias * norm_scale)[None],
        grad_in,
    )


def solution(mesh):
    in_specs = (
        P("groups", "filt", None, None, None),
        P("section", "filt", None, None),
        P("section", "filt"),
        P("groups", "filt", None, None, None),
    )
    out_specs = (
        P(("groups", "section"), "filt", None, None),
        P(("groups", "section"), "filt"),
        P(("groups", "section"), None, "filt", None, None, None),
    )
    return jax.shard_map(local, mesh=mesh, in_specs=in_specs, out_specs=out_specs, check_vma=False)
```

time: 1070 us -> 918 us (0.86)
  blocking collectives: 360 us -> 151 us
  other arithmetic: 189 us -> 29.2 us
  matrix products: 132 us -> 261 us
  waiting for transfers between devices: 36.5 us -> 131 us
  local copies, waits for them, and re-layouts: 233 us -> 210 us
  starting transfers between devices: 93.6 us -> 109 us
    conv_general_dilated x0 -> x33, matrix products: none -> 261 us  [the longest x11 195 us: conv_weight_grad(): lax.conv_general_dilated(act, slope, (1, 1, 1), PAD3, dimension_numbers=(...]
    all_gather x22 -> x11, blocking collectives: 360 us -> 151 us  [local(): full_input = lax.all_gather(own_input, 'filt', axis=1, tiled=True)]
    dot_general x77 -> x0, matrix products: 132 us -> none  [the longest x11 40.4 us: backward_tick(): jnp.einsum('krz,irz->ki', stacked, lax.all_gather(for_sending(own_input),...]
    while x253 -> x0, other arithmetic: 107 us -> none
    dot_general x11 -> x0, local copies, waits for them, and re-layouts: 104 us -> none  [forward_tick(): jnp.einsum('ki,irz->krz', columns, panel_part, preferred_element_type=jnp...]
    reduce_scatter x11, waiting for transfers between devices: 0.02 us -> 96.4 us  [local(): lax.psum_scatter(partial, 'filt', scatter_dimension=0, tiled=True)]
    dynamic_slice x55 -> x2, local copies, waits for them, and re-layouts: 65.8 us -> 2.13 us  [local(): lax.dynamic_slice_in_dim(reversed_results, section_pos, chunk_count, axis=0)]
    unnamed x17 -> x176, local copies, waits for them, and re-layouts: 4.31 us -> 58.6 us
  transfers between devices with their start and end apart: 33 -> 31, of which waited for: 22 -> 24; matrix products, arithmetic and copies ran while one was open for 12% -> 28% of each run, Pallas kernels for 0% -> 0%
where the time goes in v1:
time: 918 us; the launch traced here: 907 us
  matrix products  261 us (28%)
  local copies, waits for them, and re-layouts  210 us (23%)
  blocking collectives  151 us (16%)
  waiting for transfers between devices  131 us (14%)
  starting transfers between devices  109 us (12%)
  other arithmetic  29.2 us (3%)
  between operations  16 us (2%)
    conv_general_dilated x11, matrix products, conv_weight_grad(): lax.conv_general_dilated(act, slope, (1, 1, 1), PAD3, dimension_numbers=(...  195 us
    all_gather x11, blocking collectives, local(): full_input = lax.all_gather(own_input, 'filt', axis=1, tiled=True)  151 us
    reduce_scatter x11, waiting for transfers between devices, local(): lax.psum_scatter(partial, 'filt', scatter_dimension=0, tiled=True)  96.4 us
    ppermute x10, starting transfers between devices, local(): incoming = lax.ppermute(outgoing, 'section', forward_pairs)  66.9 us
    unnamed x176, local copies, waits for them, and re-layouts  58.6 us
    conv_general_dilated x11, matrix products, conv_forward(): lax.conv_general_dilated(act, kernel, (1, 1, 1), PAD3, dimension_numbers=...  52.9 us
    all_gather x33, local copies, waits for them, and re-layouts, local(): full_input = lax.all_gather(own_input, 'filt', axis=1, tiled=True)  43 us
    ppermute x10, starting transfers between devices, local(): incoming = lax.ppermute(input_grad, 'section', backward_pairs)  41.5 us
  transfers between devices with their start and end apart: 31, of which 24 were waited for; matrix products, arithmetic and copies ran while one was open for 28% of the time, Pallas kernels for 0%

profile of v1, /device:TPU:1, one launch (start us, length us, event | category | flops | bytes accessed | tf_op | source)
XLA Modules:
  0.0 907.3 jit_solution(9746588383378449853)
XLA Ops:
  10.6 15.3 %all_gather.33 = bf16[1,256,4,2,128]{4,2,3,0,1:T(4,128)(2,1)S(1)} all-gather(bf16[1,64,4,2,128]{4,2,3,0,1:T(4,128)(2,1)S(1)} %copy.410), channel_id=1, replica_groups=mesh['groups'=2,'section'=4,'filt'=4] {'filt'}, dimensions={1}, use_global_device_ids=true | all-gather | bytes 655360 | tf_op jit(solution)/shard_map/all_gather | solution.py:67
  27.2 4.9 multiply_convert_fusion.9
  32.5 5.1 collective-permute-start
  41.1 13.3 %all_gather.34 = bf16[1,256,4,2,128]{4,2,3,0,1:T(4,128)(2,1)S(1)} all-gather(bf16[1,64,4,2,128]{4,2,3,0,1:T(4,128)(2,1)S(1)} %copy.416), channel_id=1, replica_groups=mesh['groups'=2,'section'=4,'filt'=4] {'filt'}, dimensions={1}, use_global_device_ids=true | all-gather | bytes 655360 | tf_op jit(solution)/shard_map/all_gather | solution.py:67
  55.5 4.9 multiply_convert_fusion.8
  60.8 7.7 collective-permute-start.1
  71.6 13.6 %all_gather.35 = bf16[1,256,4,2,128]{4,2,3,0,1:T(4,128)(2,1)S(1)} all-gather(bf16[1,64,4,2,128]{4,2,3,0,1:T(4,128)(2,1)S(1)} %copy.422), channel_id=1, replica_groups=mesh['groups'=2,'section'=4,'filt'=4] {'filt'}, dimensions={1}, use_global_device_ids=true | all-gather | bytes 655360 | tf_op jit(solution)/shard_map/all_gather | solution.py:67
  86.3 4.9 multiply_convert_fusion.7
  91.6 6.6 collective-permute-start.2
  101.7 13.5 %all_gather.36 = bf16[1,256,4,2,128]{4,2,3,0,1:T(4,128)(2,1)S(1)} all-gather(bf16[1,64,4,2,128]{4,2,3,0,1:T(4,128)(2,1)S(1)} %copy.428), channel_id=1, replica_groups=mesh['groups'=2,'section'=4,'filt'=4] {'filt'}, dimensions={1}, use_global_device_ids=true | all-gather | bytes 655360 | tf_op jit(solution)/shard_map/all_gather | solution.py:67
  118.0 4.9 multiply_convert_fusion.6
  124.0 6.8 collective-permute-start.3
  136.2 13.4 %all_gather.37 = bf16[1,256,4,2,128]{4,2,3,0,1:T(4,128)(2,1)S(1)} all-gather(bf16[1,64,4,2,128]{4,2,3,0,1:T(4,128)(2,1)} %copy.434), channel_id=1, replica_groups=mesh['groups'=2,'section'=4,'filt'=4] {'filt'}, dimensions={1}, use_global_device_ids=true | all-gather | bytes 655360 | tf_op jit(solution)/shard_map/all_gather | solution.py:67
  154.1 4.9 multiply_convert_fusion.5
  160.2 7.2 collective-permute-start.4
  174.5 14.0 %all_gather.38 = bf16[1,256,4,2,128]{4,2,3,0,1:T(4,128)(2,1)S(1)} all-gather(bf16[1,64,4,2,128]{4,2,3,0,1:T(4,128)(2,1)} %copy.440), channel_id=1, replica_groups=mesh['groups'=2,'section'=4,'filt'=4] {'filt'}, dimensions={1}, use_global_device_ids=true | all-gather | bytes 655360 | tf_op jit(solution)/shard_map/all_gather | solution.py:67
  193.8 4.9 multiply_convert_fusion.4
  199.7 6.4 collective-permute-start.5
  213.2 13.4 %all_gather.39 = bf16[1,256,4,2,128]{4,2,3,0,1:T(4,128)(2,1)S(1)} all-gather(bf16[1,64,4,2,128]{4,2,3,0,1:T(4,128)(2,1)} %copy.446), channel_id=1, replica_groups=mesh['groups'=2,'section'=4,'filt'=4] {'filt'}, dimensions={1}, use_global_device_ids=true | all-gather | bytes 655360 | tf_op jit(solution)/shard_map/all_gather | solution.py:67
  231.9 4.9 multiply_convert_fusion.3
  237.9 6.7 collective-permute-start.6
  251.7 13.8 %all_gather.40 = bf16[1,256,4,2,128]{4,2,3,0,1:T(4,128)(2,1)S(1)} all-gather(bf16[1,64,4,2,128]{4,2,3,0,1:T(4,128)(2,1)} %copy.452), channel_id=1, replica_groups=mesh['groups'=2,'section'=4,'filt'=4] {'filt'}, dimensions={1}, use_global_device_ids=true | all-gather | bytes 655360 | tf_op jit(solution)/shard_map/all_gather | solution.py:67
  270.8 4.9 multiply_convert_fusion.2
  276.1 6.6 collective-permute-start.7
  288.7 13.5 %all_gather.41 = bf16[1,256,4,2,128]{4,2,3,0,1:T(4,128)(2,1)S(1)} all-gather(bf16[1,64,4,2,128]{4,2,3,0,1:T(4,128)(2,1)} %copy.458), channel_id=1, replica_groups=mesh['groups'=2,'section'=4,'filt'=4] {'filt'}, dimensions={1}, use_global_device_ids=true | all-gather | bytes 655360 | tf_op jit(solution)/shard_map/all_gather | solution.py:67
  307.4 4.9 multiply_convert_fusion.1
  313.4 6.9 collective-permute-start.8
  327.6 13.5 %all_gather.42 = bf16[1,256,4,2,128]{4,2,3,0,1:T(4,128)(2,1)S(1)} all-gather(bf16[1,64,4,2,128]{4,2,3,0,1:T(4,128)(2,1)} %copy.464), channel_id=1, replica_groups=mesh['groups'=2,'section'=4,'filt'=4] {'filt'}, dimensions={1}, use_global_device_ids=true | all-gather | bytes 655360 | tf_op jit(solution)/shard_map/all_gather | solution.py:67
  346.4 4.9 multiply_convert_fusion
  352.4 7.0 collective-permute-start.9
  366.7 13.7 %all_gather.43 = bf16[1,256,4,2,128]{4,2,3,0,1:T(4,128)(2,1)S(1)} all-gather(bf16[1,64,4,2,128]{4,2,3,0,1:T(4,128)(2,1)} %copy.470), channel_id=1, replica_groups=mesh['groups'=2,'section'=4,'filt'=4] {'filt'}, dimensions={1}, use_global_device_ids=true | all-gather | bytes 655360 | tf_op jit(solution)/shard_map/all_gather | solution.py:67
  402.2 23.8 %reduce-scatter.12.cloned.1.call-done = bf16[64,8,128]{2,0,1:T(8,128)(2,1)} async-done(((bf16[256,8,128]{2,0,1:T(8,128)(2,1)}), bf16[64,8,128]{2,0,1:T(8,128)(2,1)}) %reduce-scatter.12.cloned.1.call-update) | async-done | bytes 131088 | tf_op jit(solution)/shard_map/reduce_scatter | solution.py:95
  449.8 17.2 %reduce-scatter.14.cloned.1.call-done = bf16[64,8,128]{2,0,1:T(8,128)(2,1)} async-done(((bf16[256,8,128]{2,0,1:T(8,128)(2,1)}), bf16[64,8,128]{2,0,1:T(8,128)(2,1)}) %reduce-scatter.14.cloned.1.call-update) | async-done | bytes 131088 | tf_op jit(solution)/shard_map/reduce_scatter | solution.py:95
  490.8 17.2 %reduce-scatter.16.cloned.1.call-done = bf16[64,8,128]{2,0,1:T(8,128)(2,1)} async-done(((bf16[256,8,128]{2,0,1:T(8,128)(2,1)}), bf16[64,8,128]{2,0,1:T(8,128)(2,1)}) %reduce-scatter.16.cloned.1.call-update) | async-done | bytes 131088 | tf_op jit(solution)/shard_map/reduce_scatter | solution.py:95
  531.9 17.1 %reduce-scatter.18.cloned.1.call-done = bf16[64,8,128]{2,0,1:T(8,128)(2,1)} async-done(((bf16[256,8,128]{2,0,1:T(8,128)(2,1)}), bf16[64,8,128]{2,0,1:T(8,128)(2,1)}) %reduce-scatter.18.cloned.1.call-update) | async-done | bytes 131088 | tf_op jit(solution)/shard_map/reduce_scatter | solution.py:95
  572.3 17.2 %reduce-scatter.20.cloned.1.call-done = bf16[64,8,128]{2,0,1:T(8,128)(2,1)} async-done(((bf16[256,8,128]{2,0,1:T(8,128)(2,1)}), bf16[64,8,128]{2,0,1:T(8,128)(2,1)}) %reduce-scatter.20.cloned.1.call-update) | async-done | bytes 131088 | tf_op jit(solution)/shard_map/reduce_scatter | solution.py:95
  591.3 4.6 collective-permute-start.14
  651.8 18.0 %fusion.153 = f32[64,3,3,3,256]{4,0,3,2,1:T(8,128)} fusion(bf16[1,256,4,2,128]{1,0,4,3,2:T(2,128)(2,1)} %copy.477, bf16[1,64,4,2,128]{1,3,4,2,0:T(2,128)(2,1)S(1)} %copy-done.17), kind=kOutput, calls=%fused_computation.241 | convolution fusion | flops 500695040 | bytes 2424832 | tf_op jit(solution)/shard_map/conv_general_dilated | solution.py:36
  674.9 16.5 %fusion.151 = f32[64,3,3,3,256]{4,0,3,2,1:T(8,128)} fusion(bf16[1,256,4,2,128]{1,0,4,3,2:T(2,128)(2,1)S(1)} %copy-done.26, bf16[1,64,4,2,128]{1,3,4,2,0:T(2,128)(2,1)S(1)} %copy-done.28), kind=kOutput, calls=%fused_computation.239 | convolution fusion | flops 500695040 | bytes 2424832 | tf_op jit(solution)/shard_map/conv_general_dilated | solution.py:36
  698.8 16.8 %fusion.149 = f32[64,3,3,3,256]{4,0,3,2,1:T(8,128)} fusion(bf16[1,256,4,2,128]{1,0,4,3,2:T(2,128)(2,1)S(1)} %copy-done.25, bf16[1,64,4,2,128]{1,3,4,2,0:T(2,128)(2,1)S(1)} %copy-done.29), kind=kOutput, calls=%fused_computation.237 | convolution fusion | flops 500695040 | bytes 2424832 | tf_op jit(solution)/shard_map/conv_general_dilated | solution.py:36
  720.7 16.5 %fusion.147 = f32[64,3,3,3,256]{4,0,3,2,1:T(8,128)} fusion(bf16[1,256,4,2,128]{1,0,4,3,2:T(2,128)(2,1)S(1)} %copy-done.24, bf16[1,64,4,2,128]{1,3,4,2,0:T(2,128)(2,1)S(1)} %copy-done.30), kind=kOutput, calls=%fused_computation.235 | convolution fusion | flops 500695040 | bytes 2424832 | tf_op jit(solution)/shard_map/conv_general_dilated | solution.py:36
  744.2 16.8 %fusion.145 = f32[64,3,3,3,256]{4,0,3,2,1:T(8,128)} fusion(bf16[1,256,4,2,128]{1,0,4,3,2:T(2,128)(2,1)S(1)} %copy-done.23, bf16[1,64,4,2,128]{1,3,4,2,0:T(2,128)(2,1)S(1)} %copy-done.31), kind=kOutput, calls=%fused_computation.233 | convolution fusion | flops 500695040 | bytes 2424832 | tf_op jit(solution)/shard_map/conv_general_dilated | solution.py:36
  765.5 17.8 %fusion.143 = f32[64,3,3,3,256]{4,0,3,2,1:T(8,128)} fusion(bf16[1,256,4,2,128]{1,0,4,3,2:T(2,128)(2,1)} %copy.532, bf16[1,64,4,2,128]{1,3,4,2,0:T(2,128)(2,1)S(1)} %copy-done.32), kind=kOutput, calls=%fused_computation.231 | convolution fusion | flops 500695040 | bytes 2424832 | tf_op jit(solution)/shard_map/conv_general_dilated | solution.py:36
  789.0 16.9 %fusion.141 = f32[64,3,3,3,256]{4,0,3,2,1:T(8,128)} fusion(bf16[1,256,4,2,128]{1,0,4,3,2:T(2,128)(2,1)S(1)} %copy-done.22, bf16[1,64,4,2,128]{1,3,4,2,0:T(2,128)(2,1)S(1)} %copy-done.34), kind=kOutput, calls=%fused_computation.229 | convolution fusion | flops 500695040 | bytes 2424832 | tf_op jit(solution)/shard_map/conv_general_dilated | solution.py:36
  810.3 17.8 %fusion.139 = f32[64,3,3,3,256]{4,0,3,2,1:T(8,128)} fusion(bf16[1,256,4,2,128]{1,0,4,3,2:T(2,128)(2,1)} %copy.554, bf16[1,64,4,2,128]{1,3,4,2,0:T(2,128)(2,1)S(1)} %copy-done.36), kind=kOutput, calls=%fused_computation.227 | convolution fusion | flops 500695040 | bytes 2424832 | tf_op jit(solution)/shard_map/conv_general_dilated | solution.py:36
  833.8 16.7 %fusion.137 = f32[64,3,3,3,256]{4,0,3,2,1:T(8,128)} fusion(bf16[1,256,4,2,128]{1,0,4,3,2:T(2,128)(2,1)S(1)} %copy-done.21, bf16[1,64,4,2,128]{1,3,4,2,0:T(2,128)(2,1)S(1)} %get-tuple-element.20), kind=kOutput, calls=%fused_computation.225 | convolution fusion | flops 500695040 | bytes 2424832 | tf_op jit(solution)/shard_map/conv_general_dilated | solution.py:36
  854.9 16.5 %fusion.134 = f32[64,3,3,3,256]{4,0,3,2,1:T(8,128)} fusion(bf16[1,256,4,2,128]{1,0,4,3,2:T(2,128)(2,1)S(1)} %copy-done.19, bf16[1,64,4,2,128]{1,3,4,2,0:T(2,128)(2,1)S(1)} %get-tuple-element.24), kind=kOutput, calls=%fused_computation.222 | convolution fusion | flops 500695040 | bytes 2424832 | tf_op jit(solution)/shard_map/conv_general_dilated | solution.py:36
  871.5 24.5 %add_multiply_fusion = f32[64,3,3,3,256]{4,0,3,2,1:T(8,128)} fusion(f32[64,3,3,3,256]{4,0,3,2,1:T(8,128)} %fusion.134, f32[64,3,3,3,256]{4,0,3,2,1:T(8,128)} %fusion.137, f32[64,3,3,3,256]{4,0,3,2,1:T(8,128)} %fusion.139, f32[64,3,3,3,256]{4,0,3,2,1:T(8,128)} %fusion.141, f32[64,3,3,3,256]{4,0,3,2,1:T(8,128)} %fusion.143, f32[64,3,3,3,256]{4,0,3,2,1:T(8,128)} %fusion.145, ...), kind=kOutput, calls=%fused_computation | convolution fusion | flops 505561088 | bytes 20119552 | tf_op jit(solution)/shard_map/conv_general_dilated | solution.py:36
  (457 shorter events, 332.4 us)
Async XLA Ops:
  7.2 418.8 %reduce-scatter.12.cloned.1.call-start = ((), (), s32[]{:S(2)}) async-start(), calls=%async_computation.11 | async-start | bytes 655360 | tf_op jit(solution)/shard_map/reduce_scatter | solution.py:95
  32.5 8.4 collective-permute-start
  60.8 10.6 %collective-permute-start.1 = (bf16[1,64,4,2,128]{1,3,4,2,0:T(2,128)(2,1)S(1)}, bf16[1,64,4,2,128]{1,3,4,2,0:T(2,128)(2,1)S(1)}, u32[]{:S(2)}, u32[]{:S(2)}) collective-permute-start(bf16[1,64,4,2,128]{1,3,4,2,0:T(2,128)(2,1)S(1)} %slice_bitcast_fusion.30), channel_id=1, source_target_pairs={{0,4},{4,8},{8,12},{1,5},{5,9},{9,13},{2,6},{6,10},{10,14},{3,7},{... | collective-permute-start | bytes 393224 | tf_op jit(solution)/shard_map/ppermute | solution.py:73
  91.6 9.9 %collective-permute-start.2 = (bf16[1,64,4,2,128]{1,3,4,2,0:T(2,128)(2,1)S(1)}, bf16[1,64,4,2,128]{1,3,4,2,0:T(2,128)(2,1)S(1)}, u32[]{:S(2)}, u32[]{:S(2)}) collective-permute-start(bf16[1,64,4,2,128]{1,3,4,2,0:T(2,128)(2,1)S(1)} %slice_bitcast_fusion.29), channel_id=1, source_target_pairs={{0,4},{4,8},{8,12},{1,5},{5,9},{9,13},{2,6},{6,10},{10,14},{3,7},{... | collective-permute-start | bytes 393224 | tf_op jit(solution)/shard_map/ppermute | solution.py:73
  124.0 10.4 %collective-permute-start.3 = (bf16[1,64,4,2,128]{1,3,4,2,0:T(2,128)(2,1)}, bf16[1,64,4,2,128]{1,3,4,2,0:T(2,128)(2,1)}, u32[]{:S(2)}, u32[]{:S(2)}) collective-permute-start(bf16[1,64,4,2,128]{1,3,4,2,0:T(2,128)(2,1)} %slice_bitcast_fusion.28), channel_id=1, source_target_pairs={{0,4},{4,8},{8,12},{1,5},{5,9},{9,13},{2,6},{6,10},{10,14},{3,7},{... | collective-permute-start | bytes 393224 | tf_op jit(solution)/shard_map/ppermute | solution.py:73
  160.2 10.8 %collective-permute-start.4 = (bf16[1,64,4,2,128]{1,3,4,2,0:T(2,128)(2,1)}, bf16[1,64,4,2,128]{1,3,4,2,0:T(2,128)(2,1)}, u32[]{:S(2)}, u32[]{:S(2)}) collective-permute-start(bf16[1,64,4,2,128]{1,3,4,2,0:T(2,128)(2,1)} %slice_bitcast_fusion.27), channel_id=1, source_target_pairs={{0,4},{4,8},{8,12},{1,5},{5,9},{9,13},{2,6},{6,10},{10,14},{3,7},{... | collective-permute-start | bytes 393224 | tf_op jit(solution)/shard_map/ppermute | solution.py:73
  199.7 10.0 %collective-permute-start.5 = (bf16[1,64,4,2,128]{1,3,4,2,0:T(2,128)(2,1)}, bf16[1,64,4,2,128]{1,3,4,2,0:T(2,128)(2,1)}, u32[]{:S(2)}, u32[]{:S(2)}) collective-permute-start(bf16[1,64,4,2,128]{1,3,4,2,0:T(2,128)(2,1)} %slice_bitcast_fusion.26), channel_id=1, source_target_pairs={{0,4},{4,8},{8,12},{1,5},{5,9},{9,13},{2,6},{6,10},{10,14},{3,7},{... | collective-permute-start | bytes 393224 | tf_op jit(solution)/shard_map/ppermute | solution.py:73
  237.9 10.3 %collective-permute-start.6 = (bf16[1,64,4,2,128]{1,3,4,2,0:T(2,128)(2,1)}, bf16[1,64,4,2,128]{1,3,4,2,0:T(2,128)(2,1)}, u32[]{:S(2)}, u32[]{:S(2)}) collective-permute-start(bf16[1,64,4,2,128]{1,3,4,2,0:T(2,128)(2,1)} %slice_bitcast_fusion.25), channel_id=1, source_target_pairs={{0,4},{4,8},{8,12},{1,5},{5,9},{9,13},{2,6},{6,10},{10,14},{3,7},{... | collective-permute-start | bytes 393224 | tf_op jit(solution)/shard_map/ppermute | solution.py:73
  276.1 9.9 %collective-permute-start.7 = (bf16[1,64,4,2,128]{1,3,4,2,0:T(2,128)(2,1)S(1)}, bf16[1,64,4,2,128]{1,3,4,2,0:T(2,128)(2,1)S(1)}, u32[]{:S(2)}, u32[]{:S(2)}) collective-permute-start(bf16[1,64,4,2,128]{1,3,4,2,0:T(2,128)(2,1)S(1)} %slice_bitcast_fusion.24), channel_id=1, source_target_pairs={{0,4},{4,8},{8,12},{1,5},{5,9},{9,13},{2,6},{6,10},{10,14},{3,7},{... | collective-permute-start | bytes 393224 | tf_op jit(solution)/shard_map/ppermute | solution.py:73
  313.4 10.5 %collective-permute-start.8 = (bf16[1,64,4,2,128]{1,3,4,2,0:T(2,128)(2,1)}, bf16[1,64,4,2,128]{1,3,4,2,0:T(2,128)(2,1)}, u32[]{:S(2)}, u32[]{:S(2)}) collective-permute-start(bf16[1,64,4,2,128]{1,3,4,2,0:T(2,128)(2,1)} %slice_bitcast_fusion.23), channel_id=1, source_target_pairs={{0,4},{4,8},{8,12},{1,5},{5,9},{9,13},{2,6},{6,10},{10,14},{3,7},{... | collective-permute-start | bytes 393224 | tf_op jit(solution)/shard_map/ppermute | solution.py:73
  352.4 10.6 %collective-permute-start.9 = (bf16[1,64,4,2,128]{1,3,4,2,0:T(2,128)(2,1)}, bf16[1,64,4,2,128]{1,3,4,2,0:T(2,128)(2,1)}, u32[]{:S(2)}, u32[]{:S(2)}) collective-permute-start(bf16[1,64,4,2,128]{1,3,4,2,0:T(2,128)(2,1)} %slice_bitcast_fusion.22), channel_id=1, source_target_pairs={{0,4},{4,8},{8,12},{1,5},{5,9},{9,13},{2,6},{6,10},{10,14},{3,7},{... | collective-permute-start | bytes 393224 | tf_op jit(solution)/shard_map/ppermute | solution.py:73
  402.1 64.9 %reduce-scatter.14.cloned.1.call-start = ((), (), s32[]{:S(2)}) async-start(), calls=%async_computation.12 | async-start | bytes 655360 | tf_op jit(solution)/shard_map/reduce_scatter | solution.py:95
  427.8 9.6 %collective-permute-start.10 = (bf16[1,64,4,2,128]{1,3,4,2,0:T(2,128)(2,1)}, bf16[1,64,4,2,128]{1,3,4,2,0:T(2,128)(2,1)}, u32[]{:S(2)}, u32[]{:S(2)}) collective-permute-start(bf16[1,64,4,2,128]{1,3,4,2,0:T(2,128)(2,1)} %copy.486), channel_id=1, source_target_pairs={{4,0},{8,4},{12,8},{5,1},{9,5},{13,9},{6,2},{10,6},{14,10},{7,3},{... | collective-permute-start | bytes 393224 | tf_op jit(solution)/shard_map/ppermute | solution.py:99
  449.8 58.3 %reduce-scatter.16.cloned.1.call-start = ((), (), s32[]{:S(2)}) async-start(), calls=%async_computation.13 | async-start | bytes 655360 | tf_op jit(solution)/shard_map/reduce_scatter | solution.py:95
  468.8 9.6 %collective-permute-start.11 = (bf16[1,64,4,2,128]{1,3,4,2,0:T(2,128)(2,1)}, bf16[1,64,4,2,128]{1,3,4,2,0:T(2,128)(2,1)}, u32[]{:S(2)}, u32[]{:S(2)}) collective-permute-start(bf16[1,64,4,2,128]{1,3,4,2,0:T(2,128)(2,1)} %copy.497), channel_id=1, source_target_pairs={{4,0},{8,4},{12,8},{5,1},{9,5},{13,9},{6,2},{10,6},{14,10},{7,3},{... | collective-permute-start | bytes 393224 | tf_op jit(solution)/shard_map/ppermute | solution.py:99
  490.8 58.2 %reduce-scatter.18.cloned.1.call-start = ((), (), s32[]{:S(2)}) async-start(), calls=%async_computation.14 | async-start | bytes 655360 | tf_op jit(solution)/shard_map/reduce_scatter | solution.py:95
  509.8 9.6 %collective-permute-start.12 = (bf16[1,64,4,2,128]{1,3,4,2,0:T(2,128)(2,1)}, bf16[1,64,4,2,128]{1,3,4,2,0:T(2,128)(2,1)}, u32[]{:S(2)}, u32[]{:S(2)}) collective-permute-start(bf16[1,64,4,2,128]{1,3,4,2,0:T(2,128)(2,1)} %copy.508), channel_id=1, source_target_pairs={{4,0},{8,4},{12,8},{5,1},{9,5},{13,9},{6,2},{10,6},{14,10},{7,3},{... | collective-permute-start | bytes 393224 | tf_op jit(solution)/shard_map/ppermute | solution.py:99
  531.9 57.6 %reduce-scatter.20.cloned.1.call-start = ((), (), s32[]{:S(2)}) async-start(), calls=%async_computation.15 | async-start | bytes 655360 | tf_op jit(solution)/shard_map/reduce_scatter | solution.py:95
  550.8 9.6 %collective-permute-start.13 = (bf16[1,64,4,2,128]{1,3,4,2,0:T(2,128)(2,1)}, bf16[1,64,4,2,128]{1,3,4,2,0:T(2,128)(2,1)}, u32[]{:S(2)}, u32[]{:S(2)}) collective-permute-start(bf16[1,64,4,2,128]{1,3,4,2,0:T(2,128)(2,1)} %copy.519), channel_id=1, source_target_pairs={{4,0},{8,4},{12,8},{5,1},{9,5},{13,9},{6,2},{10,6},{14,10},{7,3},{... | collective-permute-start | bytes 393224 | tf_op jit(solution)/shard_map/ppermute | solution.py:99
  572.3 76.2 %reduce-scatter.22.cloned.1.call-start = ((), (), s32[]{:S(2)}) async-start(), calls=%async_computation.16 | async-start | bytes 655360 | tf_op jit(solution)/shard_map/reduce_scatter | solution.py:95
  591.3 9.6 %collective-permute-start.14 = (bf16[1,64,4,2,128]{1,3,4,2,0:T(2,128)(2,1)}, bf16[1,64,4,2,128]{1,3,4,2,0:T(2,128)(2,1)}, u32[]{:S(2)}, u32[]{:S(2)}) collective-permute-start(bf16[1,64,4,2,128]{1,3,4,2,0:T(2,128)(2,1)} %copy.530), channel_id=1, source_target_pairs={{4,0},{8,4},{12,8},{5,1},{9,5},{13,9},{6,2},{10,6},{14,10},{7,3},{... | collective-permute-start | bytes 393224 | tf_op jit(solution)/shard_map/ppermute | solution.py:99
  612.8 80.6 %reduce-scatter.24.cloned.1.call-start = ((), (), s32[]{:S(2)}) async-start(), calls=%async_computation.17 | async-start | bytes 655360 | tf_op jit(solution)/shard_map/reduce_scatter | solution.py:95
  649.5 20.2 %collective-permute-start.15 = (bf16[1,64,4,2,128]{1,3,4,2,0:T(2,128)(2,1)S(1)}, bf16[1,64,4,2,128]{1,3,4,2,0:T(2,128)(2,1)S(1)}, u32[]{:S(2)}, u32[]{:S(2)}) collective-permute-start(bf16[1,64,4,2,128]{1,3,4,2,0:T(2,128)(2,1)S(1)} %copy.541), channel_id=1, source_target_pairs={{4,0},{8,4},{12,8},{5,1},{9,5},{13,9},{6,2},{10,6},{14,10},{7,3},{... | collective-permute-start | bytes 393224 | tf_op jit(solution)/shard_map/ppermute | solution.py:99
  674.8 24.1 %copy-start.25 = (bf16[1,256,4,2,128]{1,0,4,3,2:T(2,128)(2,1)S(1)}, bf16[1,256,4,2,128]{1,0,4,3,2:T(2,128)(2,1)}, u32[]{:S(2)}) copy-start(bf16[1,256,4,2,128]{1,0,4,3,2:T(2,128)(2,1)} %copy.499) | copy-start | bytes 1572868
  674.8 24.1 %copy-start.29 = (bf16[1,64,4,2,128]{1,3,4,2,0:T(2,128)(2,1)S(1)}, bf16[1,64,4,2,128]{1,3,4,2,0:T(2,128)(2,1)}, u32[]{:S(2)}) copy-start(bf16[1,64,4,2,128]{1,3,4,2,0:T(2,128)(2,1)} %get-tuple-element.8) | copy-start | bytes 393220
  674.8 63.9 %reduce-scatter.26.cloned.1.call-start = ((), (), s32[]{:S(2)}) async-start(), calls=%async_computation.18 | async-start | bytes 655360 | tf_op jit(solution)/shard_map/reduce_scatter | solution.py:95
  694.5 21.2 %collective-permute-start.16 = (bf16[1,64,4,2,128]{1,3,4,2,0:T(2,128)(2,1)S(1)}, bf16[1,64,4,2,128]{1,3,4,2,0:T(2,128)(2,1)S(1)}, u32[]{:S(2)}, u32[]{:S(2)}) collective-permute-start(bf16[1,64,4,2,128]{1,3,4,2,0:T(2,128)(2,1)S(1)} %copy.552), channel_id=1, source_target_pairs={{4,0},{8,4},{12,8},{5,1},{9,5},{13,9},{6,2},{10,6},{14,10},{7,3},{... | collective-permute-start | bytes 393224 | tf_op jit(solution)/shard_map/ppermute | solution.py:99
  720.7 23.5 %copy-start.23 = (bf16[1,256,4,2,128]{1,0,4,3,2:T(2,128)(2,1)S(1)}, bf16[1,256,4,2,128]{1,0,4,3,2:T(2,128)(2,1)}, u32[]{:S(2)}) copy-start(bf16[1,256,4,2,128]{1,0,4,3,2:T(2,128)(2,1)} %copy.521) | copy-start | bytes 1572868
  720.7 23.5 %copy-start.31 = (bf16[1,64,4,2,128]{1,3,4,2,0:T(2,128)(2,1)S(1)}, bf16[1,64,4,2,128]{1,3,4,2,0:T(2,128)(2,1)}, u32[]{:S(2)}) copy-start(bf16[1,64,4,2,128]{1,3,4,2,0:T(2,128)(2,1)} %get-tuple-element.12) | copy-start | bytes 393220
  720.7 62.8 %reduce-scatter.28.cloned.1.call-start = ((), (), s32[]{:S(2)}) async-start(), calls=%async_computation.19 | async-start | bytes 655360 | tf_op jit(solution)/shard_map/reduce_scatter | solution.py:95
  739.8 21.2 %copy-start.15 = (f32[4,2,8,17,64]{4,1,3,2,0:T(2,128)S(1)}, f32[4,2,8,17,64]{4,1,3,2,0:T(2,128)}, u32[]{:S(2)}) copy-start(f32[4,2,8,17,64]{4,1,3,2,0:T(2,128)} %copy.563) | copy-start | bytes 835588
  739.8 21.2 %collective-permute-start.17 = (bf16[1,64,4,2,128]{1,3,4,2,0:T(2,128)(2,1)S(1)}, bf16[1,64,4,2,128]{1,3,4,2,0:T(2,128)(2,1)S(1)}, u32[]{:S(2)}, u32[]{:S(2)}) collective-permute-start(bf16[1,64,4,2,128]{1,3,4,2,0:T(2,128)(2,1)S(1)} %copy.562), channel_id=1, source_target_pairs={{4,0},{8,4},{12,8},{5,1},{9,5},{13,9},{6,2},{10,6},{14,10},{7,3},{... | collective-permute-start | bytes 393224 | tf_op jit(solution)/shard_map/ppermute | solution.py:99
  765.4 23.5 %copy-start.22 = (bf16[1,256,4,2,128]{1,0,4,3,2:T(2,128)(2,1)S(1)}, bf16[1,256,4,2,128]{1,0,4,3,2:T(2,128)(2,1)}, u32[]{:S(2)}) copy-start(bf16[1,256,4,2,128]{1,0,4,3,2:T(2,128)(2,1)} %copy.543) | copy-start | bytes 1572868
  765.4 23.5 %copy-start.34 = (bf16[1,64,4,2,128]{1,3,4,2,0:T(2,128)(2,1)S(1)}, bf16[1,64,4,2,128]{1,3,4,2,0:T(2,128)(2,1)}, u32[]{:S(2)}) copy-start(bf16[1,64,4,2,128]{1,3,4,2,0:T(2,128)(2,1)} %copy-done.33) | copy-start | bytes 393220
  765.4 62.9 %reduce-scatter.30.cloned.1.call-start = ((), (), s32[]{:S(2)}) async-start(), calls=%async_computation.20 | async-start | bytes 655360 | tf_op jit(solution)/shard_map/reduce_scatter | solution.py:95
  784.6 21.2 %copy-start.14 = (f32[4,2,8,17,64]{4,1,3,2,0:T(2,128)S(1)}, f32[4,2,8,17,64]{4,1,3,2,0:T(2,128)}, u32[]{:S(2)}) copy-start(f32[4,2,8,17,64]{4,1,3,2,0:T(2,128)} %copy.573) | copy-start | bytes 835588
  784.6 21.2 %collective-permute-start.18 = (bf16[1,64,4,2,128]{1,3,4,2,0:T(2,128)(2,1)S(1)}, bf16[1,64,4,2,128]{1,3,4,2,0:T(2,128)(2,1)S(1)}, u32[]{:S(2)}, u32[]{:S(2)}) collective-permute-start(bf16[1,64,4,2,128]{1,3,4,2,0:T(2,128)(2,1)S(1)} %copy.572), channel_id=1, source_target_pairs={{4,0},{8,4},{12,8},{5,1},{9,5},{13,9},{6,2},{10,6},{14,10},{7,3},{... | collective-permute-start | bytes 393224 | tf_op jit(solution)/shard_map/ppermute | solution.py:99
  810.2 23.5 %copy-start.21 = (bf16[1,256,4,2,128]{1,0,4,3,2:T(2,128)(2,1)S(1)}, bf16[1,256,4,2,128]{1,0,4,3,2:T(2,128)(2,1)}, u32[]{:S(2)}) copy-start(bf16[1,256,4,2,128]{1,0,4,3,2:T(2,128)(2,1)} %copy.564) | copy-start | bytes 1572868
  810.2 86.4 %reduce-scatter.32.cloned.1.call-start = ((), (), s32[]{:S(2)}) async-start(), calls=%async_computation.21 | async-start | bytes 655360 | tf_op jit(solution)/shard_map/reduce_scatter | solution.py:95
  829.4 21.1 %collective-permute-start.19 = (bf16[1,64,4,2,128]{1,3,4,2,0:T(2,128)(2,1)S(1)}, bf16[1,64,4,2,128]{1,3,4,2,0:T(2,128)(2,1)S(1)}, u32[]{:S(2)}, u32[]{:S(2)}) collective-permute-start(bf16[1,64,4,2,128]{1,3,4,2,0:T(2,128)(2,1)S(1)} %copy.582), channel_id=1, source_target_pairs={{4,0},{8,4},{12,8},{5,1},{9,5},{13,9},{6,2},{10,6},{14,10},{7,3},{... | collective-permute-start | bytes 393224 | tf_op jit(solution)/shard_map/ppermute | solution.py:99
  871.4 24.6 %copy-start.58 = (f32[64]{0:T(128)S(1)}, f32[64]{0:T(128)}, u32[]{:S(2)}) copy-start(f32[64]{0:T(128)} %get-tuple-element.5) | copy-start | bytes 772
  871.4 24.6 %copy-start.59 = (f32[64]{0:T(128)S(1)}, f32[64]{0:T(128)}, u32[]{:S(2)}) copy-start(f32[64]{0:T(128)} %get-tuple-element.3) | copy-start | bytes 772
  871.4 24.6 %copy-start.60 = (f32[64]{0:T(128)S(1)}, f32[64]{0:T(128)}, u32[]{:S(2)}) copy-start(f32[64]{0:T(128)} %get-tuple-element.7) | copy-start | bytes 772
  871.4 24.7 %copy-start.61 = (f32[64]{0:T(128)S(1)}, f32[64]{0:T(128)}, u32[]{:S(2)}) copy-start(f32[64]{0:T(128)} %get-tuple-element.9) | copy-start | bytes 772
  871.4 26.1 %copy-start.57 = (bf16[64,8,128]{2,0,1:T(8,128)(2,1)S(1)}, bf16[64,8,128]{2,0,1:T(8,128)(2,1)}, u32[]{:S(2)}) copy-start(bf16[64,8,128]{2,0,1:T(8,128)(2,1)} %reduce-scatter.30.cloned.1.call-done) | copy-start | bytes 393220
  871.4 26.1 %copy-start.56 = (bf16[64,8,128]{2,0,1:T(8,128)(2,1)S(1)}, bf16[64,8,128]{2,0,1:T(8,128)(2,1)}, u32[]{:S(2)}) copy-start(bf16[64,8,128]{2,0,1:T(8,128)(2,1)} %reduce-scatter.28.cloned.1.call-done) | copy-start | bytes 393220
  871.4 26.2 %copy-start.55 = (bf16[64,8,128]{2,0,1:T(8,128)(2,1)S(1)}, bf16[64,8,128]{2,0,1:T(8,128)(2,1)}, u32[]{:S(2)}) copy-start(bf16[64,8,128]{2,0,1:T(8,128)(2,1)} %reduce-scatter.26.cloned.1.call-done) | copy-start | bytes 393220
  871.5 26.2 %copy-start.54 = (bf16[64,8,128]{2,0,1:T(8,128)(2,1)S(1)}, bf16[64,8,128]{2,0,1:T(8,128)(2,1)}, u32[]{:S(2)}) copy-start(bf16[64,8,128]{2,0,1:T(8,128)(2,1)} %reduce-scatter.24.cloned.1.call-done) | copy-start | bytes 393220
  (47 other events, 236.2 us)
Sparse Core Ops, SparseCore 0:
  402.3 23.6 reduce-scatter.11
  449.9 17.0 reduce-scatter.13
  490.9 17.0 reduce-scatter.15
  532.0 16.9 reduce-scatter.17
  572.4 17.0 reduce-scatter.19
  612.9 16.9 reduce-scatter.21
  674.9 18.4 reduce-scatter.23
  720.8 17.8 reduce-scatter.25
  765.5 17.9 reduce-scatter.27
  810.3 17.9 reduce-scatter.29
  855.0 17.8 reduce-scatter.31

commit v2 on v1

v2 whole, which is shorter than its diff:
```python
import functools
import math

import jax
import jax.numpy as jnp
from jax import lax
from jax.experimental import pallas as pl
from jax.experimental.pallas import tpu as pltpu
from jax.sharding import PartitionSpec as P

CHUNK = 1


def lane_shift(values, step, row_len):
    if step == 0:
        return values
    width = values.shape[-1]
    wide = values.astype(jnp.float32)
    rolled = pltpu.roll(wide, (-step) % width, 1)
    z = lax.broadcasted_iota(jnp.int32, values.shape, 1) % row_len
    keep = (z + step >= 0) & (z + step < row_len)
    return jnp.where(keep, rolled, 0.0).astype(values.dtype)


def block_source(block, step_x, step_y, extent_x, extent_y):
    pos_x, pos_y = block // extent_y + step_x, block % extent_y + step_y
    if 0 <= pos_x < extent_x and 0 <= pos_y < extent_y:
        return pos_x * extent_y + pos_y
    return None


def forward_kernel(extent, chunk, act_ref, w_ref, b_ref, out_ref):
    extent_x, extent_y, row_len = extent
    blocks = extent_x * extent_y
    cells = blocks * row_len
    own = out_ref.shape[0]
    for n in range(chunk):
        act = act_ref[:, n * cells:(n + 1) * cells]
        acc = [None] * blocks
        for c_index, step_z in enumerate((-1, 0, 1)):
            shifted = lane_shift(act, step_z, row_len)
            product = jnp.dot(w_ref[c_index], shifted, preferred_element_type=jnp.float32)
            for a_index, step_x in enumerate((-1, 0, 1)):
                for b_index, step_y in enumerate((-1, 0, 1)):
                    rows = (a_index * 3 + b_index) * own
                    for block in range(blocks):
                        src = block_source(block, step_x, step_y, extent_x, extent_y)
                        if src is None:
                            continue
                        piece = product[rows:rows + own, src * row_len:(src + 1) * row_len]
                        acc[block] = piece if acc[block] is None else acc[block] + piece
        total = jnp.concatenate(acc, axis=1) + b_ref[...]
        out_ref[:, n * cells:(n + 1) * cells] = total


def backward_kernel(extent, chunk, slope_ref, act_ref, w_ref, acc_ref, gin_ref, gw_ref, stack_ref):
    extent_x, extent_y, row_len = extent
    blocks = extent_x * extent_y
    cells = blocks * row_len
    own = slope_ref.shape[0]
    gw = acc_ref[...]
    zero_block = jnp.zeros((own, row_len), stack_ref.dtype)
    for n in range(chunk):
        slope = slope_ref[:, n * cells:(n + 1) * cells]
        for c_index, step_z in enumerate((-1, 0, 1)):
            shifted = lane_shift(slope, -step_z, row_len)
            for a_index, step_x in enumerate((-1, 0, 1)):
                for b_index, step_y in enumerate((-1, 0, 1)):
                    tap = a_index * 9 + b_index * 3 + c_index
                    pieces = []
                    for block in range(blocks):
                        src = block_source(block, -step_x, -step_y, extent_x, extent_y)
                        if src is None:
                            pieces.append(zero_block)
                        else:
                            pieces.append(shifted[:, src * row_len:(src + 1) * row_len])
                    stack_ref[tap * own:(tap + 1) * own, :] = jnp.concatenate(pieces, axis=1)
        stacked = stack_ref[...]
        gin_ref[:, n * cells:(n + 1) * cells] = jnp.dot(
            w_ref[...], stacked, preferred_element_type=jnp.float32
        ).astype(gin_ref.dtype)
        gw = gw + lax.dot_general(
            stacked, act_ref[:, n * cells:(n + 1) * cells], (((1,), (1,)), ((), ())),
            preferred_element_type=jnp.float32,
        )
    gw_ref[...] = gw


def conv_forward_call(act, w_fwd, bias_col, extent, chunk):
    own = bias_col.shape[0]
    return pl.pallas_call(
        functools.partial(forward_kernel, extent, chunk),
        out_shape=jax.ShapeDtypeStruct((own, act.shape[1]), jnp.float32),
        compiler_params=pltpu.CompilerParams(vmem_limit_bytes=48 * 1024 * 1024),
    )(act, w_fwd, bias_col)


def conv_backward_call(slope, act, w_bwd, acc, extent, chunk):
    own = slope.shape[0]
    channels = act.shape[0]
    cells = extent[0] * extent[1] * extent[2]
    return pl.pallas_call(
        functools.partial(backward_kernel, extent, chunk),
        out_shape=(
            jax.ShapeDtypeStruct((channels, act.shape[1]), jnp.bfloat16),
            jax.ShapeDtypeStruct(acc.shape, jnp.float32),
        ),
        scratch_shapes=[pltpu.VMEM((27 * own, cells), jnp.bfloat16)],
        input_output_aliases={3: 1},
        compiler_params=pltpu.CompilerParams(vmem_limit_bytes=48 * 1024 * 1024),
    )(slope, act, w_bwd, acc)

def take_blocks(values, axis, order):
    count = order.shape[0]
    shape = values.shape
    split = shape[:axis] + (count, shape[axis] // count) + shape[axis + 1:]
    picked = jnp.take(values.reshape(split), order, axis=axis)
    return picked.reshape(shape)


RING_LIMIT = 4


def ring_gather(value, count):
    if count > RING_LIMIT:
        return lax.all_gather(value, "filt", axis=0, tiled=True)
    pieces = [value]
    for step in range(1, count):
        pieces.append(lax.ppermute(value, "filt", [(j, (j + step) % count) for j in range(count)]))
    return jnp.concatenate(pieces, axis=0)


def ring_scatter_sum(partial, count):
    if count > RING_LIMIT:
        return lax.psum_scatter(partial, "filt", scatter_dimension=0, tiled=True)
    rows = partial.shape[0] // count
    total = partial[:rows].astype(jnp.float32)
    for step in range(1, count):
        piece = partial[step * rows:(step + 1) * rows].astype(jnp.bfloat16)
        total = total + lax.ppermute(
            piece, "filt", [(j, (j + step) % count) for j in range(count)]
        ).astype(jnp.float32)
    return total.astype(jnp.bfloat16)


def silu_slope(pre_act):
    sigmoid = jax.nn.sigmoid(pre_act)
    return sigmoid * (1.0 + pre_act * (1.0 - sigmoid))


def local(volumes, weights, biases, cotangent):
    section_count = lax.axis_size("section")
    section_pos = lax.axis_index("section")
    micro_count = volumes.shape[0]
    chunk = CHUNK if micro_count % CHUNK == 0 else 1
    chunk_count = micro_count // chunk
    tick_count = chunk_count + section_count - 1
    own_count, tap_count, channels = weights.shape[1:]
    extent = tuple(volumes.shape[2:])
    cells = extent[0] * extent[1] * extent[2]
    width = chunk * cells
    weight = weights[0]
    w_fwd = jnp.transpose(weight.reshape(own_count, 3, 3, 3, channels), (3, 1, 2, 0, 4)).reshape(
        3, 9 * own_count, channels
    )
    w_bwd = jnp.transpose(weight, (2, 1, 0)).reshape(channels, tap_count * own_count)
    filt_count = lax.axis_size("filt")
    filt_pos = lax.axis_index("filt")
    if filt_count > RING_LIMIT:
        back_order = jnp.arange(filt_count)
        ahead_order = jnp.arange(filt_count)
    else:
        back_order = (filt_pos - jnp.arange(filt_count)) % filt_count
        ahead_order = (filt_pos + jnp.arange(filt_count)) % filt_count
    w_fwd = take_blocks(w_fwd, 2, back_order)
    w_bwd = take_blocks(w_bwd, 0, ahead_order)
    bias_col = biases[0][:, None]
    flat_volumes = jnp.transpose(volumes.reshape(micro_count, own_count, cells), (1, 0, 2)).reshape(
        own_count, micro_count * cells
    )
    flat_cotangent = jnp.transpose(
        cotangent.reshape(micro_count, own_count, cells), (1, 0, 2)
    ).reshape(own_count, micro_count * cells)
    slab = (own_count, width)
    forward_pairs = [(i, i + 1) for i in range(section_count - 1)]
    backward_pairs = [(i + 1, i) for i in range(section_count - 1)]

    incoming = jnp.zeros(slab, jnp.bfloat16)
    gathered = []
    pres = []
    for tick in range(tick_count):
        if tick < chunk_count:
            first = flat_volumes[:, tick * width:(tick + 1) * width]
        else:
            first = jnp.zeros(slab, jnp.bfloat16)
        own_input = jnp.where(section_pos == 0, first, incoming)
        full_input = ring_gather(own_input, filt_count)
        pre_act = conv_forward_call(full_input, w_fwd, bias_col, extent, chunk)
        gathered.append(full_input)
        pres.append(pre_act)
        if tick < tick_count - 1:
            outgoing = jax.nn.silu(pre_act).astype(jnp.bfloat16)
            incoming = lax.ppermute(outgoing, "section", forward_pairs)

    incoming = jnp.zeros(slab, jnp.bfloat16)
    grad_rows = jnp.zeros((tap_count * own_count, channels), jnp.float32)
    grad_bias = jnp.zeros((own_count,), jnp.float32)
    results = []
    for tick in range(tick_count):
        forward_tick = tick_count - 1 - tick
        if tick < chunk_count:
            start = (chunk_count - 1 - tick) * width
            last = flat_cotangent[:, start:start + width]
        else:
            last = jnp.zeros(slab, jnp.bfloat16)
        upstream = jnp.where(section_pos == section_count - 1, last, incoming)
        sample = forward_tick - section_pos
        in_range = (sample >= 0) & (sample < chunk_count)
        slope = (upstream.astype(jnp.float32) * silu_slope(pres[forward_tick])).astype(jnp.bfloat16)
        slope = jnp.where(in_range, slope, jnp.zeros((), jnp.bfloat16))
        grad_bias = grad_bias + jnp.sum(slope.astype(jnp.float32), axis=1)
        partial, grad_rows = conv_backward_call(
            slope, gathered[forward_tick], w_bwd, grad_rows, extent, chunk
        )
        input_grad = ring_scatter_sum(partial, filt_count)
        results.append(input_grad)
        if tick < tick_count - 1:
            incoming = lax.ppermute(input_grad, "section", backward_pairs)

    stacked_results = jnp.stack(results[::-1]).reshape(tick_count, own_count, chunk, cells)
    stacked_results = jnp.transpose(stacked_results, (0, 2, 1, 3))
    picked = lax.dynamic_slice_in_dim(stacked_results, section_pos, chunk_count, axis=0)
    grad_in = picked.reshape((1, micro_count, own_count) + extent)
    norm_scale = 1.0 / math.sqrt(micro_count * cells)
    grad_rows = take_blocks(grad_rows, 1, back_order)
    grad_kernel = jnp.transpose(grad_rows.reshape(tap_count, own_count, channels), (1, 0, 2))
    return (
        (grad_kernel * norm_scale)[None],
        (grad_bias * norm_scale)[None],
        grad_in,
    )


def solution(mesh):
    in_specs = (
        P("groups", "filt", None, None, None),
        P("section", "filt", None, None),
        P("section", "filt"),
        P("groups", "filt", None, None, None),
    )
    out_specs = (
        P(("groups", "section"), "filt", None, None),
        P(("groups", "section"), "filt"),
        P(("groups", "section"), None, "filt", None, None, None),
    )
    return jax.shard_map(local, mesh=mesh, in_specs=in_specs, out_specs=out_specs, check_vma=False)
```

time: 918 us -> 500 us (0.54)
  matrix products: 261 us -> 0 us
  local copies, waits for them, and re-layouts: 210 us -> 59 us
  blocking collectives: 151 us -> 0 us
  waiting for transfers between devices: 131 us -> 200 us
  starting transfers between devices: 109 us -> 163 us
  Pallas kernels: 0 us -> 37.7 us
  between operations: 16 us -> 2.18 us
    conv_general_dilated x33 -> x0, matrix products: 261 us -> none  [the longest x11 195 us: conv_weight_grad(): lax.conv_general_dilated(act, slope, (1, 1, 1), PAD3, dimension_numbers=(...]
    all_gather x11 -> x0, blocking collectives: 151 us -> none  [local(): full_input = lax.all_gather(own_input, 'filt', axis=1, tiled=True)]
    ppermute x0 -> x66, waiting for transfers between devices: none -> 140 us  [the longest x33 75.5 us: ring_gather(): lax.ppermute(value, 'filt', [(j, (j + step) % count) for j in range(count)])]
    ppermute x0 -> x66, starting transfers between devices: none -> 102 us  [the longest x33 56.7 us: ring_scatter_sum(): lax.ppermute(piece, 'filt', [(j, (j + step) % count) for j in range(count)])]
    reduce_scatter x11 -> x0, waiting for transfers between devices: 96.4 us -> none  [local(): lax.psum_scatter(partial, 'filt', scatter_dimension=0, tiled=True)]
    all_gather x33 -> x0, local copies, waits for them, and re-layouts: 43 us -> none  [local(): full_input = lax.all_gather(own_input, 'filt', axis=1, tiled=True)]
    convert_element_type x53 -> x0, local copies, waits for them, and re-layouts: 38.9 us -> none  [the longest x33 30.7 us: local(): conv_input_grad(slope, kernel).astype(jnp.bfloat16)]
    pallas_call x0 -> x22, Pallas kernels: none -> 37.7 us  [the longest x11 24.2 us: conv_backward_call(): pl.pallas_call(functools.partial(backward_kernel, extent, chunk), out_sha...]
  transfers between devices with their start and end apart: 31 -> 86, of which waited for: 24 -> 75; matrix products, arithmetic and copies ran while one was open for 28% -> 6% of each run, Pallas kernels for 0% -> 0%
where the time goes in v2:
time: 500 us; the launch traced here: 490 us
  waiting for transfers between devices  200 us (40%)
  starting transfers between devices  163 us (33%)
  local copies, waits for them, and re-layouts  59 us (12%)
  Pallas kernels  37.7 us (8%)
  other arithmetic  28.6 us (6%)
    ppermute x33, waiting for transfers between devices, ring_gather(): lax.ppermute(value, 'filt', [(j, (j + step) % count) for j in range(count)])  75.5 us
    ppermute x33, waiting for transfers between devices, ring_scatter_sum(): lax.ppermute(piece, 'filt', [(j, (j + step) % count) for j in range(count)])  64.1 us
    ppermute x33, starting transfers between devices, ring_scatter_sum(): lax.ppermute(piece, 'filt', [(j, (j + step) % count) for j in range(count)])  56.7 us
    ppermute x33, starting transfers between devices, ring_gather(): lax.ppermute(value, 'filt', [(j, (j + step) % count) for j in range(count)])  44.9 us
    ppermute x10, waiting for transfers between devices, local(): incoming = lax.ppermute(input_grad, 'section', backward_pairs)  43 us
    ppermute x10, starting transfers between devices, local(): incoming = lax.ppermute(outgoing, 'section', forward_pairs)  38.3 us
    unnamed x77, local copies, waits for them, and re-layouts  27.9 us
    pallas_call x11, Pallas kernels, conv_backward_call(): pl.pallas_call(functools.partial(backward_kernel, extent, chunk), out_sha...  24.2 us
  transfers between devices with their start and end apart: 86, of which 75 were waited for; matrix products, arithmetic and copies ran while one was open for 6% of the time, Pallas kernels for 0%

profile of v2, /device:TPU:1, one launch (start us, length us, event | category | flops | bytes accessed | tf_op | source)
XLA Modules:
  0.0 490.0 jit_solution(16931135067867092052)
XLA Ops:
  19.7 3.6 collective-permute-start.3
  33.2 3.9 collective-permute-done.5
  39.5 4.3 collective-permute-start.7
  51.6 3.8 collective-permute-done.8
  55.4 4.2 collective-permute-done.9
  61.8 3.3 collective-permute-start.11
  70.4 3.8 collective-permute-done.12
  74.2 4.3 collective-permute-done.13
  80.6 3.1 collective-permute-start.15
  92.7 4.7 collective-permute-done.17
  99.6 3.9 collective-permute-start.19
  109.3 3.3 collective-permute-done.20
  112.6 4.4 collective-permute-done.21
  119.5 3.7 collective-permute-start.23
  132.3 4.3 collective-permute-done.25
  139.2 3.7 collective-permute-start.27
  148.7 3.2 collective-permute-done.28
  152.0 4.1 collective-permute-done.29
  158.6 4.1 collective-permute-start.31
  168.5 3.2 collective-permute-done.32
  171.7 4.0 collective-permute-done.33
  178.1 4.2 collective-permute-start.35
  188.2 3.2 collective-permute-done.36
  191.4 3.8 collective-permute-done.37
  197.7 4.3 collective-permute-start.39
  232.0 6.2 %collective-permute-done.44 = bf16[64,1024]{1,0:T(8,128)(2,1)S(1)} collective-permute-done((bf16[64,1024]{1,0:T(8,128)(2,1)S(1)}, bf16[64,1024]{1,0:T(8,128)(2,1)S(1)}, u32[]{:S(2)}, u32[]{:S(2)}) %collective-permute-start.44) | collective-permute-done | bytes 131104 | tf_op jit(solution)/shard_map/ppermute | solution.py:140
  241.6 3.9 collective-permute-done.46
  250.1 3.1 collective-permute-start.47
  257.7 3.9 collective-permute-done.48
  265.0 4.5 collective-permute-done.50
  281.3 3.6 collective-permute-done.52
  287.9 4.6 collective-permute-done.54
  304.3 3.8 collective-permute-done.56
  311.2 4.4 collective-permute-done.58
  327.5 3.9 collective-permute-done.60
  334.4 4.3 collective-permute-done.62
  350.7 3.9 collective-permute-done.64
  357.9 4.1 collective-permute-done.66
  373.9 3.9 collective-permute-done.68
  380.9 4.3 collective-permute-done.70
  397.2 3.9 collective-permute-done.72
  404.2 4.3 collective-permute-done.74
  420.4 3.9 collective-permute-done.76
  427.4 4.3 collective-permute-done.78
  436.2 3.1 collective-permute-start.79
  443.6 3.9 collective-permute-done.80
  450.6 4.3 collective-permute-done.82
  472.0 3.6 gather.23
  (320 shorter events, 297.7 us)
Async XLA Ops:
  3.2 12.0 %collective-permute-start = (bf16[64,1024]{1,0:T(8,128)(2,1)}, bf16[64,1024]{1,0:T(8,128)(2,1)}, u32[]{:S(2)}, u32[]{:S(2)}) collective-permute-start(bf16[64,1024]{1,0:T(8,128)(2,1)} %slice_select_fusion), channel_id=1, source_target_pairs={{0,1},{1,2},{2,3},{3,0},{4,5},{5,6},{6,7},{7,4},{8,9},{9,10},{10,1... | collective-permute-start | bytes 393224 | tf_op jit(solution)/shard_map/ppermute | solution.py:129
  5.3 11.9 %collective-permute-start.1 = (bf16[64,1024]{1,0:T(8,128)(2,1)}, bf16[64,1024]{1,0:T(8,128)(2,1)}, u32[]{:S(2)}, u32[]{:S(2)}) collective-permute-start(bf16[64,1024]{1,0:T(8,128)(2,1)} %slice_select_fusion), channel_id=1, source_target_pairs={{0,2},{1,3},{2,0},{3,1},{4,6},{5,7},{6,4},{7,5},{8,10},{9,11},{10,... | collective-permute-start | bytes 393224 | tf_op jit(solution)/shard_map/ppermute | solution.py:129
  7.6 9.6 %collective-permute-start.2 = (bf16[64,1024]{1,0:T(8,128)(2,1)}, bf16[64,1024]{1,0:T(8,128)(2,1)}, u32[]{:S(2)}, u32[]{:S(2)}) collective-permute-start(bf16[64,1024]{1,0:T(8,128)(2,1)} %slice_select_fusion), channel_id=1, source_target_pairs={{0,3},{1,0},{2,1},{3,2},{4,7},{5,4},{6,5},{7,6},{8,11},{9,8},{10,9... | collective-permute-start | bytes 393224 | tf_op jit(solution)/shard_map/ppermute | solution.py:129
  25.2 7.9 %collective-permute-start.4 = (bf16[64,1024]{1,0:T(8,128)(2,1)S(1)}, bf16[64,1024]{1,0:T(8,128)(2,1)S(1)}, u32[]{:S(2)}, u32[]{:S(2)}) collective-permute-start(bf16[64,1024]{1,0:T(8,128)(2,1)S(1)} %slice_select_fusion.1), channel_id=1, source_target_pairs={{0,1},{1,2},{2,3},{3,0},{4,5},{5,6},{6,7},{7,4},{8,9},{9,10},{10,1... | collective-permute-start | bytes 393224 | tf_op jit(solution)/shard_map/ppermute | solution.py:129
  28.3 8.8 %collective-permute-start.5 = (bf16[64,1024]{1,0:T(8,128)(2,1)S(1)}, bf16[64,1024]{1,0:T(8,128)(2,1)S(1)}, u32[]{:S(2)}, u32[]{:S(2)}) collective-permute-start(bf16[64,1024]{1,0:T(8,128)(2,1)S(1)} %slice_select_fusion.1), channel_id=1, source_target_pairs={{0,2},{1,3},{2,0},{3,1},{4,6},{5,7},{6,4},{7,5},{8,10},{9,11},{10,... | collective-permute-start | bytes 393224 | tf_op jit(solution)/shard_map/ppermute | solution.py:129
  29.6 7.7 %collective-permute-start.6 = (bf16[64,1024]{1,0:T(8,128)(2,1)S(1)}, bf16[64,1024]{1,0:T(8,128)(2,1)S(1)}, u32[]{:S(2)}, u32[]{:S(2)}) collective-permute-start(bf16[64,1024]{1,0:T(8,128)(2,1)S(1)} %slice_select_fusion.1), channel_id=1, source_target_pairs={{0,3},{1,0},{2,1},{3,2},{4,7},{5,4},{6,5},{7,6},{8,11},{9,8},{10,9... | collective-permute-start | bytes 393224 | tf_op jit(solution)/shard_map/ppermute | solution.py:129
  48.3 11.3 %collective-permute-start.9 = (bf16[64,1024]{1,0:T(8,128)(2,1)S(1)}, bf16[64,1024]{1,0:T(8,128)(2,1)S(1)}, u32[]{:S(2)}, u32[]{:S(2)}) collective-permute-start(bf16[64,1024]{1,0:T(8,128)(2,1)S(1)} %slice_select_fusion.2), channel_id=1, source_target_pairs={{0,2},{1,3},{2,0},{3,1},{4,6},{5,7},{6,4},{7,5},{8,10},{9,11},{10,... | collective-permute-start | bytes 393224 | tf_op jit(solution)/shard_map/ppermute | solution.py:129
  67.1 11.3 %collective-permute-start.13 = (bf16[64,1024]{1,0:T(8,128)(2,1)S(1)}, bf16[64,1024]{1,0:T(8,128)(2,1)S(1)}, u32[]{:S(2)}, u32[]{:S(2)}) collective-permute-start(bf16[64,1024]{1,0:T(8,128)(2,1)S(1)} %slice_select_fusion.3), channel_id=1, source_target_pairs={{0,2},{1,3},{2,0},{3,1},{4,6},{5,7},{6,4},{7,5},{8,10},{9,11},{10,... | collective-permute-start | bytes 393224 | tf_op jit(solution)/shard_map/ppermute | solution.py:129
  69.2 9.2 %collective-permute-start.14 = (bf16[64,1024]{1,0:T(8,128)(2,1)S(1)}, bf16[64,1024]{1,0:T(8,128)(2,1)S(1)}, u32[]{:S(2)}, u32[]{:S(2)}) collective-permute-start(bf16[64,1024]{1,0:T(8,128)(2,1)S(1)} %slice_select_fusion.3), channel_id=1, source_target_pairs={{0,3},{1,0},{2,1},{3,2},{4,7},{5,4},{6,5},{7,6},{8,11},{9,8},{10,9... | collective-permute-start | bytes 393224 | tf_op jit(solution)/shard_map/ppermute | solution.py:129
  87.7 9.8 %collective-permute-start.17 = (bf16[64,1024]{1,0:T(8,128)(2,1)S(1)}, bf16[64,1024]{1,0:T(8,128)(2,1)S(1)}, u32[]{:S(2)}, u32[]{:S(2)}) collective-permute-start(bf16[64,1024]{1,0:T(8,128)(2,1)S(1)} %slice_select_fusion.4), channel_id=1, source_target_pairs={{0,2},{1,3},{2,0},{3,1},{4,6},{5,7},{6,4},{7,5},{8,10},{9,11},{10,... | collective-permute-start | bytes 393224 | tf_op jit(solution)/shard_map/ppermute | solution.py:129
  89.2 8.2 %collective-permute-start.18 = (bf16[64,1024]{1,0:T(8,128)(2,1)S(1)}, bf16[64,1024]{1,0:T(8,128)(2,1)S(1)}, u32[]{:S(2)}, u32[]{:S(2)}) collective-permute-start(bf16[64,1024]{1,0:T(8,128)(2,1)S(1)} %slice_select_fusion.4), channel_id=1, source_target_pairs={{0,3},{1,0},{2,1},{3,2},{4,7},{5,4},{6,5},{7,6},{8,11},{9,8},{10,9... | collective-permute-start | bytes 393224 | tf_op jit(solution)/shard_map/ppermute | solution.py:129
  107.2 9.8 %collective-permute-start.21 = (bf16[64,1024]{1,0:T(8,128)(2,1)S(1)}, bf16[64,1024]{1,0:T(8,128)(2,1)S(1)}, u32[]{:S(2)}, u32[]{:S(2)}) collective-permute-start(bf16[64,1024]{1,0:T(8,128)(2,1)S(1)} %slice_select_fusion.5), channel_id=1, source_target_pairs={{0,2},{1,3},{2,0},{3,1},{4,6},{5,7},{6,4},{7,5},{8,10},{9,11},{10,... | collective-permute-start | bytes 393224 | tf_op jit(solution)/shard_map/ppermute | solution.py:129
  108.2 9.2 %collective-permute-start.22 = (bf16[64,1024]{1,0:T(8,128)(2,1)S(1)}, bf16[64,1024]{1,0:T(8,128)(2,1)S(1)}, u32[]{:S(2)}, u32[]{:S(2)}) collective-permute-start(bf16[64,1024]{1,0:T(8,128)(2,1)S(1)} %slice_select_fusion.5), channel_id=1, source_target_pairs={{0,3},{1,0},{2,1},{3,2},{4,7},{5,4},{6,5},{7,6},{8,11},{9,8},{10,9... | collective-permute-start | bytes 393224 | tf_op jit(solution)/shard_map/ppermute | solution.py:129
  126.9 9.7 %collective-permute-start.25 = (bf16[64,1024]{1,0:T(8,128)(2,1)S(1)}, bf16[64,1024]{1,0:T(8,128)(2,1)S(1)}, u32[]{:S(2)}, u32[]{:S(2)}) collective-permute-start(bf16[64,1024]{1,0:T(8,128)(2,1)S(1)} %slice_select_fusion.6), channel_id=1, source_target_pairs={{0,2},{1,3},{2,0},{3,1},{4,6},{5,7},{6,4},{7,5},{8,10},{9,11},{10,... | collective-permute-start | bytes 393224 | tf_op jit(solution)/shard_map/ppermute | solution.py:129
  127.9 9.1 %collective-permute-start.26 = (bf16[64,1024]{1,0:T(8,128)(2,1)S(1)}, bf16[64,1024]{1,0:T(8,128)(2,1)S(1)}, u32[]{:S(2)}, u32[]{:S(2)}) collective-permute-start(bf16[64,1024]{1,0:T(8,128)(2,1)S(1)} %slice_select_fusion.6), channel_id=1, source_target_pairs={{0,3},{1,0},{2,1},{3,2},{4,7},{5,4},{6,5},{7,6},{8,11},{9,8},{10,9... | collective-permute-start | bytes 393224 | tf_op jit(solution)/shard_map/ppermute | solution.py:129
  146.6 9.5 %collective-permute-start.29 = (bf16[64,1024]{1,0:T(8,128)(2,1)S(1)}, bf16[64,1024]{1,0:T(8,128)(2,1)S(1)}, u32[]{:S(2)}, u32[]{:S(2)}) collective-permute-start(bf16[64,1024]{1,0:T(8,128)(2,1)S(1)} %slice_select_fusion.7), channel_id=1, source_target_pairs={{0,2},{1,3},{2,0},{3,1},{4,6},{5,7},{6,4},{7,5},{8,10},{9,11},{10,... | collective-permute-start | bytes 393224 | tf_op jit(solution)/shard_map/ppermute | solution.py:129
  147.6 8.8 %collective-permute-start.30 = (bf16[64,1024]{1,0:T(8,128)(2,1)S(1)}, bf16[64,1024]{1,0:T(8,128)(2,1)S(1)}, u32[]{:S(2)}, u32[]{:S(2)}) collective-permute-start(bf16[64,1024]{1,0:T(8,128)(2,1)S(1)} %slice_select_fusion.7), channel_id=1, source_target_pairs={{0,3},{1,0},{2,1},{3,2},{4,7},{5,4},{6,5},{7,6},{8,11},{9,8},{10,9... | collective-permute-start | bytes 393224 | tf_op jit(solution)/shard_map/ppermute | solution.py:129
  166.3 9.4 %collective-permute-start.33 = (bf16[64,1024]{1,0:T(8,128)(2,1)S(1)}, bf16[64,1024]{1,0:T(8,128)(2,1)S(1)}, u32[]{:S(2)}, u32[]{:S(2)}) collective-permute-start(bf16[64,1024]{1,0:T(8,128)(2,1)S(1)} %broadcast_select_fusion.3), channel_id=1, source_target_pairs={{0,2},{1,3},{2,0},{3,1},{4,6},{5,7},{6,4},{7,5},{8,10},{9,11},{10,... | collective-permute-start | bytes 393224 | tf_op jit(solution)/shard_map/ppermute | solution.py:129
  167.3 8.6 %collective-permute-start.34 = (bf16[64,1024]{1,0:T(8,128)(2,1)S(1)}, bf16[64,1024]{1,0:T(8,128)(2,1)S(1)}, u32[]{:S(2)}, u32[]{:S(2)}) collective-permute-start(bf16[64,1024]{1,0:T(8,128)(2,1)S(1)} %broadcast_select_fusion.3), channel_id=1, source_target_pairs={{0,3},{1,0},{2,1},{3,2},{4,7},{5,4},{6,5},{7,6},{8,11},{9,8},{10,9... | collective-permute-start | bytes 393224 | tf_op jit(solution)/shard_map/ppermute | solution.py:129
  186.0 9.2 %collective-permute-start.37 = (bf16[64,1024]{1,0:T(8,128)(2,1)S(1)}, bf16[64,1024]{1,0:T(8,128)(2,1)S(1)}, u32[]{:S(2)}, u32[]{:S(2)}) collective-permute-start(bf16[64,1024]{1,0:T(8,128)(2,1)S(1)} %broadcast_select_fusion.2), channel_id=1, source_target_pairs={{0,2},{1,3},{2,0},{3,1},{4,6},{5,7},{6,4},{7,5},{8,10},{9,11},{10,... | collective-permute-start | bytes 393224 | tf_op jit(solution)/shard_map/ppermute | solution.py:129
  187.0 8.6 %collective-permute-start.38 = (bf16[64,1024]{1,0:T(8,128)(2,1)S(1)}, bf16[64,1024]{1,0:T(8,128)(2,1)S(1)}, u32[]{:S(2)}, u32[]{:S(2)}) collective-permute-start(bf16[64,1024]{1,0:T(8,128)(2,1)S(1)} %broadcast_select_fusion.2), channel_id=1, source_target_pairs={{0,3},{1,0},{2,1},{3,2},{4,7},{5,4},{6,5},{7,6},{8,11},{9,8},{10,9... | collective-permute-start | bytes 393224 | tf_op jit(solution)/shard_map/ppermute | solution.py:129
  197.7 10.7 %collective-permute-start.39 = (bf16[64,1024]{1,0:T(8,128)(2,1)S(1)}, bf16[64,1024]{1,0:T(8,128)(2,1)S(1)}, u32[]{:S(2)}, u32[]{:S(2)}) collective-permute-start(bf16[64,1024]{1,0:T(8,128)(2,1)S(1)} %multiply_convert_fusion.11), channel_id=1, source_target_pairs={{0,4},{4,8},{8,12},{1,5},{5,9},{9,13},{2,6},{6,10},{10,14},{3,7},{... | collective-permute-start | bytes 393224 | tf_op jit(solution)/shard_map/ppermute | solution.py:203
  208.4 10.1 %collective-permute-start.40 = (bf16[64,1024]{1,0:T(8,128)(2,1)S(1)}, bf16[64,1024]{1,0:T(8,128)(2,1)S(1)}, u32[]{:S(2)}, u32[]{:S(2)}) collective-permute-start(bf16[64,1024]{1,0:T(8,128)(2,1)S(1)} %broadcast_select_fusion.1), channel_id=1, source_target_pairs={{0,1},{1,2},{2,3},{3,0},{4,5},{5,6},{6,7},{7,4},{8,9},{9,10},{10,1... | collective-permute-start | bytes 393224 | tf_op jit(solution)/shard_map/ppermute | solution.py:129
  210.1 9.9 %collective-permute-start.41 = (bf16[64,1024]{1,0:T(8,128)(2,1)S(1)}, bf16[64,1024]{1,0:T(8,128)(2,1)S(1)}, u32[]{:S(2)}, u32[]{:S(2)}) collective-permute-start(bf16[64,1024]{1,0:T(8,128)(2,1)S(1)} %broadcast_select_fusion.1), channel_id=1, source_target_pairs={{0,2},{1,3},{2,0},{3,1},{4,6},{5,7},{6,4},{7,5},{8,10},{9,11},{10,... | collective-permute-start | bytes 393224 | tf_op jit(solution)/shard_map/ppermute | solution.py:129
  211.2 9.1 %collective-permute-start.42 = (bf16[64,1024]{1,0:T(8,128)(2,1)S(1)}, bf16[64,1024]{1,0:T(8,128)(2,1)S(1)}, u32[]{:S(2)}, u32[]{:S(2)}) collective-permute-start(bf16[64,1024]{1,0:T(8,128)(2,1)S(1)} %broadcast_select_fusion.1), channel_id=1, source_target_pairs={{0,3},{1,0},{2,1},{3,2},{4,7},{5,4},{6,5},{7,6},{8,11},{9,8},{10,9... | collective-permute-start | bytes 393224 | tf_op jit(solution)/shard_map/ppermute | solution.py:129
  228.0 10.2 %collective-permute-start.44 = (bf16[64,1024]{1,0:T(8,128)(2,1)S(1)}, bf16[64,1024]{1,0:T(8,128)(2,1)S(1)}, u32[]{:S(2)}, u32[]{:S(2)}) collective-permute-start(bf16[64,1024]{1,0:T(8,128)(2,1)S(1)} %get-tuple-element.101), channel_id=1, source_target_pairs={{0,2},{1,3},{2,0},{3,1},{4,6},{5,7},{6,4},{7,5},{8,10},{9,11},{10,... | collective-permute-start | bytes 393224 | tf_op jit(solution)/shard_map/ppermute | solution.py:140
  228.9 9.3 %collective-permute-start.45 = (bf16[64,1024]{1,0:T(8,128)(2,1)S(1)}, bf16[64,1024]{1,0:T(8,128)(2,1)S(1)}, u32[]{:S(2)}, u32[]{:S(2)}) collective-permute-start(bf16[64,1024]{1,0:T(8,128)(2,1)S(1)} %get-tuple-element.100), channel_id=1, source_target_pairs={{0,3},{1,0},{2,1},{3,2},{4,7},{5,4},{6,5},{7,6},{8,11},{9,8},{10,9... | collective-permute-start | bytes 393224 | tf_op jit(solution)/shard_map/ppermute | solution.py:140
  250.1 7.6 %collective-permute-start.47 = (bf16[64,1024]{1,0:T(8,128)(2,1)S(1)}, bf16[64,1024]{1,0:T(8,128)(2,1)S(1)}, u32[]{:S(2)}, u32[]{:S(2)}) collective-permute-start(bf16[64,1024]{1,0:T(8,128)(2,1)S(1)} %get-tuple-element.96), channel_id=1, source_target_pairs={{0,1},{1,2},{2,3},{3,0},{4,5},{5,6},{6,7},{7,4},{8,9},{9,10},{10,1... | collective-permute-start | bytes 393224 | tf_op jit(solution)/shard_map/ppermute | solution.py:140
  253.2 8.4 %collective-permute-start.48 = (bf16[64,1024]{1,0:T(8,128)(2,1)S(1)}, bf16[64,1024]{1,0:T(8,128)(2,1)S(1)}, u32[]{:S(2)}, u32[]{:S(2)}) collective-permute-start(bf16[64,1024]{1,0:T(8,128)(2,1)S(1)} %get-tuple-element.98), channel_id=1, source_target_pairs={{0,2},{1,3},{2,0},{3,1},{4,6},{5,7},{6,4},{7,5},{8,10},{9,11},{10,... | collective-permute-start | bytes 393224 | tf_op jit(solution)/shard_map/ppermute | solution.py:140
  254.2 8.0 %collective-permute-start.49 = (bf16[64,1024]{1,0:T(8,128)(2,1)S(1)}, bf16[64,1024]{1,0:T(8,128)(2,1)S(1)}, u32[]{:S(2)}, u32[]{:S(2)}) collective-permute-start(bf16[64,1024]{1,0:T(8,128)(2,1)S(1)} %get-tuple-element.97), channel_id=1, source_target_pairs={{0,3},{1,0},{2,1},{3,2},{4,7},{5,4},{6,5},{7,6},{8,11},{9,8},{10,9... | collective-permute-start | bytes 393224 | tf_op jit(solution)/shard_map/ppermute | solution.py:140
  276.7 8.2 %collective-permute-start.52 = (bf16[64,1024]{1,0:T(8,128)(2,1)S(1)}, bf16[64,1024]{1,0:T(8,128)(2,1)S(1)}, u32[]{:S(2)}, u32[]{:S(2)}) collective-permute-start(bf16[64,1024]{1,0:T(8,128)(2,1)S(1)} %get-tuple-element.95), channel_id=1, source_target_pairs={{0,2},{1,3},{2,0},{3,1},{4,6},{5,7},{6,4},{7,5},{8,10},{9,11},{10,... | collective-permute-start | bytes 393224 | tf_op jit(solution)/shard_map/ppermute | solution.py:140
  299.9 8.2 %collective-permute-start.56 = (bf16[64,1024]{1,0:T(8,128)(2,1)S(1)}, bf16[64,1024]{1,0:T(8,128)(2,1)S(1)}, u32[]{:S(2)}, u32[]{:S(2)}) collective-permute-start(bf16[64,1024]{1,0:T(8,128)(2,1)S(1)} %get-tuple-element.92), channel_id=1, source_target_pairs={{0,2},{1,3},{2,0},{3,1},{4,6},{5,7},{6,4},{7,5},{8,10},{9,11},{10,... | collective-permute-start | bytes 393224 | tf_op jit(solution)/shard_map/ppermute | solution.py:140
  300.8 7.5 %collective-permute-start.57 = (bf16[64,1024]{1,0:T(8,128)(2,1)S(1)}, bf16[64,1024]{1,0:T(8,128)(2,1)S(1)}, u32[]{:S(2)}, u32[]{:S(2)}) collective-permute-start(bf16[64,1024]{1,0:T(8,128)(2,1)S(1)} %get-tuple-element.91), channel_id=1, source_target_pairs={{0,3},{1,0},{2,1},{3,2},{4,7},{5,4},{6,5},{7,6},{8,11},{9,8},{10,9... | collective-permute-start | bytes 393224 | tf_op jit(solution)/shard_map/ppermute | solution.py:140
  323.1 8.2 %collective-permute-start.60 = (bf16[64,1024]{1,0:T(8,128)(2,1)S(1)}, bf16[64,1024]{1,0:T(8,128)(2,1)S(1)}, u32[]{:S(2)}, u32[]{:S(2)}) collective-permute-start(bf16[64,1024]{1,0:T(8,128)(2,1)S(1)} %get-tuple-element.89), channel_id=1, source_target_pairs={{0,2},{1,3},{2,0},{3,1},{4,6},{5,7},{6,4},{7,5},{8,10},{9,11},{10,... | collective-permute-start | bytes 393224 | tf_op jit(solution)/shard_map/ppermute | solution.py:140
  324.0 7.5 %collective-permute-start.61 = (bf16[64,1024]{1,0:T(8,128)(2,1)S(1)}, bf16[64,1024]{1,0:T(8,128)(2,1)S(1)}, u32[]{:S(2)}, u32[]{:S(2)}) collective-permute-start(bf16[64,1024]{1,0:T(8,128)(2,1)S(1)} %get-tuple-element.88), channel_id=1, source_target_pairs={{0,3},{1,0},{2,1},{3,2},{4,7},{5,4},{6,5},{7,6},{8,11},{9,8},{10,9... | collective-permute-start | bytes 393224 | tf_op jit(solution)/shard_map/ppermute | solution.py:140
  346.4 8.2 %collective-permute-start.64 = (bf16[64,1024]{1,0:T(8,128)(2,1)S(1)}, bf16[64,1024]{1,0:T(8,128)(2,1)S(1)}, u32[]{:S(2)}, u32[]{:S(2)}) collective-permute-start(bf16[64,1024]{1,0:T(8,128)(2,1)S(1)} %get-tuple-element.86), channel_id=1, source_target_pairs={{0,2},{1,3},{2,0},{3,1},{4,6},{5,7},{6,4},{7,5},{8,10},{9,11},{10,... | collective-permute-start | bytes 393224 | tf_op jit(solution)/shard_map/ppermute | solution.py:140
  347.2 7.5 %collective-permute-start.65 = (bf16[64,1024]{1,0:T(8,128)(2,1)S(1)}, bf16[64,1024]{1,0:T(8,128)(2,1)S(1)}, u32[]{:S(2)}, u32[]{:S(2)}) collective-permute-start(bf16[64,1024]{1,0:T(8,128)(2,1)S(1)} %get-tuple-element.85), channel_id=1, source_target_pairs={{0,3},{1,0},{2,1},{3,2},{4,7},{5,4},{6,5},{7,6},{8,11},{9,8},{10,9... | collective-permute-start | bytes 393224 | tf_op jit(solution)/shard_map/ppermute | solution.py:140
  369.6 8.2 %collective-permute-start.68 = (bf16[64,1024]{1,0:T(8,128)(2,1)S(1)}, bf16[64,1024]{1,0:T(8,128)(2,1)S(1)}, u32[]{:S(2)}, u32[]{:S(2)}) collective-permute-start(bf16[64,1024]{1,0:T(8,128)(2,1)S(1)} %get-tuple-element.83), channel_id=1, source_target_pairs={{0,2},{1,3},{2,0},{3,1},{4,6},{5,7},{6,4},{7,5},{8,10},{9,11},{10,... | collective-permute-start | bytes 393224 | tf_op jit(solution)/shard_map/ppermute | solution.py:140
  370.4 7.5 %collective-permute-start.69 = (bf16[64,1024]{1,0:T(8,128)(2,1)S(1)}, bf16[64,1024]{1,0:T(8,128)(2,1)S(1)}, u32[]{:S(2)}, u32[]{:S(2)}) collective-permute-start(bf16[64,1024]{1,0:T(8,128)(2,1)S(1)} %get-tuple-element.82), channel_id=1, source_target_pairs={{0,3},{1,0},{2,1},{3,2},{4,7},{5,4},{6,5},{7,6},{8,11},{9,8},{10,9... | collective-permute-start | bytes 393224 | tf_op jit(solution)/shard_map/ppermute | solution.py:140
  392.9 8.2 %collective-permute-start.72 = (bf16[64,1024]{1,0:T(8,128)(2,1)S(1)}, bf16[64,1024]{1,0:T(8,128)(2,1)S(1)}, u32[]{:S(2)}, u32[]{:S(2)}) collective-permute-start(bf16[64,1024]{1,0:T(8,128)(2,1)S(1)} %get-tuple-element.80), channel_id=1, source_target_pairs={{0,2},{1,3},{2,0},{3,1},{4,6},{5,7},{6,4},{7,5},{8,10},{9,11},{10,... | collective-permute-start | bytes 393224 | tf_op jit(solution)/shard_map/ppermute | solution.py:140
  393.7 7.5 %collective-permute-start.73 = (bf16[64,1024]{1,0:T(8,128)(2,1)S(1)}, bf16[64,1024]{1,0:T(8,128)(2,1)S(1)}, u32[]{:S(2)}, u32[]{:S(2)}) collective-permute-start(bf16[64,1024]{1,0:T(8,128)(2,1)S(1)} %get-tuple-element.79), channel_id=1, source_target_pairs={{0,3},{1,0},{2,1},{3,2},{4,7},{5,4},{6,5},{7,6},{8,11},{9,8},{10,9... | collective-permute-start | bytes 393224 | tf_op jit(solution)/shard_map/ppermute | solution.py:140
  416.1 8.2 %collective-permute-start.76 = (bf16[64,1024]{1,0:T(8,128)(2,1)S(1)}, bf16[64,1024]{1,0:T(8,128)(2,1)S(1)}, u32[]{:S(2)}, u32[]{:S(2)}) collective-permute-start(bf16[64,1024]{1,0:T(8,128)(2,1)S(1)} %get-tuple-element.77), channel_id=1, source_target_pairs={{0,2},{1,3},{2,0},{3,1},{4,6},{5,7},{6,4},{7,5},{8,10},{9,11},{10,... | collective-permute-start | bytes 393224 | tf_op jit(solution)/shard_map/ppermute | solution.py:140
  416.9 7.5 %collective-permute-start.77 = (bf16[64,1024]{1,0:T(8,128)(2,1)S(1)}, bf16[64,1024]{1,0:T(8,128)(2,1)S(1)}, u32[]{:S(2)}, u32[]{:S(2)}) collective-permute-start(bf16[64,1024]{1,0:T(8,128)(2,1)S(1)} %get-tuple-element.76), channel_id=1, source_target_pairs={{0,3},{1,0},{2,1},{3,2},{4,7},{5,4},{6,5},{7,6},{8,11},{9,8},{10,9... | collective-permute-start | bytes 393224 | tf_op jit(solution)/shard_map/ppermute | solution.py:140
  439.3 8.2 %collective-permute-start.80 = (bf16[64,1024]{1,0:T(8,128)(2,1)S(1)}, bf16[64,1024]{1,0:T(8,128)(2,1)S(1)}, u32[]{:S(2)}, u32[]{:S(2)}) collective-permute-start(bf16[64,1024]{1,0:T(8,128)(2,1)S(1)} %get-tuple-element.74), channel_id=1, source_target_pairs={{0,2},{1,3},{2,0},{3,1},{4,6},{5,7},{6,4},{7,5},{8,10},{9,11},{10,... | collective-permute-start | bytes 393224 | tf_op jit(solution)/shard_map/ppermute | solution.py:140
  440.1 7.5 %collective-permute-start.81 = (bf16[64,1024]{1,0:T(8,128)(2,1)S(1)}, bf16[64,1024]{1,0:T(8,128)(2,1)S(1)}, u32[]{:S(2)}, u32[]{:S(2)}) collective-permute-start(bf16[64,1024]{1,0:T(8,128)(2,1)S(1)} %get-tuple-element.73), channel_id=1, source_target_pairs={{0,3},{1,0},{2,1},{3,2},{4,7},{5,4},{6,5},{7,6},{8,11},{9,8},{10,9... | collective-permute-start | bytes 393224 | tf_op jit(solution)/shard_map/ppermute | solution.py:140
  459.8 17.8 %collective-permute-start.83 = (bf16[64,1024]{1,0:T(8,128)(2,1)}, bf16[64,1024]{1,0:T(8,128)(2,1)}, u32[]{:S(2)}, u32[]{:S(2)}) collective-permute-start(bf16[64,1024]{1,0:T(8,128)(2,1)} %get-tuple-element.69), channel_id=1, source_target_pairs={{0,1},{1,2},{2,3},{3,0},{4,5},{5,6},{6,7},{7,4},{8,9},{9,10},{10,1... | collective-permute-start | bytes 393224 | tf_op jit(solution)/shard_map/ppermute | solution.py:140
  462.8 14.8 %collective-permute-start.84 = (bf16[64,1024]{1,0:T(8,128)(2,1)}, bf16[64,1024]{1,0:T(8,128)(2,1)}, u32[]{:S(2)}, u32[]{:S(2)}) collective-permute-start(bf16[64,1024]{1,0:T(8,128)(2,1)} %get-tuple-element.71), channel_id=1, source_target_pairs={{0,2},{1,3},{2,0},{3,1},{4,6},{5,7},{6,4},{7,5},{8,10},{9,11},{10,... | collective-permute-start | bytes 393224 | tf_op jit(solution)/shard_map/ppermute | solution.py:140
  463.6 14.0 %collective-permute-start.85 = (bf16[64,1024]{1,0:T(8,128)(2,1)}, bf16[64,1024]{1,0:T(8,128)(2,1)}, u32[]{:S(2)}, u32[]{:S(2)}) collective-permute-start(bf16[64,1024]{1,0:T(8,128)(2,1)} %get-tuple-element.70), channel_id=1, source_target_pairs={{0,3},{1,0},{2,1},{3,2},{4,7},{5,4},{6,5},{7,6},{8,11},{9,8},{10,9... | collective-permute-start | bytes 393224 | tf_op jit(solution)/shard_map/ppermute | solution.py:140
  (71 other events, 453.5 us)
